TPU v7x, 512 devices: a whole 4x4x16 slice. The times are simulated.
512 devices in a mesh: dp: 16 (over z), owner: 32 (over x, y, core).
Axes of the slice: x: 4, y: 4, z: 16, core: 2. Of those that a mesh axis runs over, the one named last changes fastest.
Arguments:
- tokens: bfloat16 [65536, 8192], P(('dp', 'owner')), may hold values from -6 to 6
- residual: bfloat16 [65536, 8192], P(('dp', 'owner')), may hold values from -6 to 6
- token_adapter_index: int32 [65536, 1], P(('dp', 'owner')), may hold values from 0 to 31; in each aligned block of 128 rows (0 to 127, 128 to 255, ...) at most 6 rows name the same one
- adapter_down_weight: bfloat16 [32, 64, 8192], P('owner', None, 'dp'), may hold values from -0.0625 to 0.0625
- adapter_up_weight: bfloat16 [32, 64, 8192], P('owner', None, 'dp'), may hold values from -0.75 to 0.75
- down_moment_first: bfloat16 [32, 64, 8192], P('owner', None, 'dp'), may hold values from -270 to 270
- down_moment_second: bfloat16 [32, 64, 8192], P('owner', None, 'dp'), may hold values from 816 to 24576
- up_moment_first: bfloat16 [32, 64, 8192], P('owner', None, 'dp'), may hold values from -27.125 to 27.125
- up_moment_second: bfloat16 [32, 64, 8192], P('owner', None, 'dp'), may hold values from 6.125 to 204
Outputs:
- down_update: float32 [32, 64, 8192], P('owner', None, 'dp')
- up_update: float32 [32, 64, 8192], P('owner', None, 'dp')
- token_loss: float32 [65536], P(('dp', 'owner'))
Inputs may be any that keep to these rules, and one draw needn't show every extreme that they name: `token_adapter_index`: of the 128 rows of one device, at most 6 name one adapter, and in some devices one adapter is named by exactly 6.
All inputs are finite; a program needn't handle non-finite values.
Results may differ from a plain program's by a relative error of at most 0.0091.
Values may be sent and summed in bfloat16 or wider, within the bound.
No kernel may reach another device: no remote copies, remote signals or barrier semaphores. Data moves between devices by JAX's collectives and lax.ppermute only.
A program may use at most 128 MiB of HBM per device.

v0:
```python
import jax
import jax.numpy as jnp
from jax import lax
from jax.sharding import PartitionSpec as P

adapter_scale = 0.5
adam_eps = 1e-08


def adam_update(grad, first, second):
    first_new = 0.9 * first.astype(jnp.float32) + 0.1 * grad
    second_new = 0.95 * second.astype(jnp.float32) + 0.05 * grad * grad
    return first_new / (jnp.sqrt(second_new) + adam_eps)


def body(
    tokens,
    residual,
    token_adapter_index,
    adapter_down_weight,
    adapter_up_weight,
    down_moment_first,
    down_moment_second,
    up_moment_first,
    up_moment_second,
):
    owner_index = lax.axis_size("owner")
    tok_rows = tokens.shape[0]
    model_width_value = tokens.shape[1]
    column_span = adapter_down_weight.shape[2]
    slot_capacity = max(2, 3 * tok_rows // (2 * owner_index))
    route_ids = token_adapter_index[:, 0]
    member = (route_ids[:, None] == jnp.arange(owner_index, dtype=jnp.int32)[None, :]).astype(
        jnp.int32
    )
    before = jnp.cumsum(member, axis=0) - member
    within = jnp.sum(before * member, axis=1)
    target = route_ids * slot_capacity + within
    dispatch = (
        jnp.arange(owner_index * slot_capacity, dtype=jnp.int32)[:, None] == target[None, :]
    ).astype(jnp.bfloat16)

    def placed_rows(row_block):
        return jnp.dot(dispatch, row_block, preferred_element_type=jnp.float32).astype(jnp.bfloat16)

    down_full, up_weight_whole = (
        lax.all_gather(adapter_down_weight, "dp", axis=2, tiled=True),
        lax.all_gather(adapter_up_weight, "dp", axis=2, tiled=True),
    )
    down_full = down_full[0]
    up_weight_whole = up_weight_whole[0]

    def spread(row_block):
        return placed_rows(row_block).reshape(owner_index, slot_capacity, model_width_value)

    arrived = lax.all_to_all(
        spread(tokens), "owner", split_axis=0, concat_axis=0, tiled=True
    ).reshape(owner_index * slot_capacity, model_width_value)
    hidden_state = lax.dot_general(
        arrived, down_full, (((1,), (1,)), ((), ())), preferred_element_type=jnp.float32
    ).astype(jnp.bfloat16)
    adapter_output = (
        adapter_scale * jnp.dot(hidden_state, up_weight_whole, preferred_element_type=jnp.float32)
    ).astype(jnp.bfloat16)
    hidden_state, adapter_output = (hidden_state, adapter_output)
    returned = lax.all_to_all(
        adapter_output.reshape(owner_index, slot_capacity, model_width_value),
        "owner",
        split_axis=0,
        concat_axis=0,
        tiled=True,
    )
    returned = returned.reshape(owner_index * slot_capacity, model_width_value)
    adapter_home_index = lax.dot_general(
        dispatch, returned, (((0,), (0,)), ((), ())), preferred_element_type=jnp.float32
    )
    shifted_index = residual.astype(jnp.float32) + adapter_home_index
    token_loss = jnp.mean(0.5 * shifted_index * shifted_index, axis=1)
    output_gradient = lax.all_to_all(
        spread(shifted_index.astype(jnp.bfloat16)), "owner", split_axis=0, concat_axis=0, tiled=True
    )
    output_gradient = output_gradient.reshape(owner_index * slot_capacity, model_width_value)
    up_gradient = adapter_scale * lax.dot_general(
        hidden_state, output_gradient, (((0,), (0,)), ((), ())), preferred_element_type=jnp.float32
    )
    hidden_gradient = (
        adapter_scale
        * lax.dot_general(
            output_gradient,
            up_weight_whole,
            (((1,), (1,)), ((), ())),
            preferred_element_type=jnp.float32,
        )
    ).astype(jnp.bfloat16)
    down_grad = lax.dot_general(
        hidden_gradient, arrived, (((0,), (0,)), ((), ())), preferred_element_type=jnp.float32
    )
    summed_down, summed_up = lax.psum((down_grad, up_gradient), "dp")
    offset = lax.axis_index("dp") * column_span
    down_share = lax.dynamic_slice_in_dim(summed_down, offset, column_span, 1)
    up_share = lax.dynamic_slice_in_dim(summed_up, offset, column_span, 1)
    down_update = adam_update(down_share, down_moment_first[0], down_moment_second[0])
    up_update = adam_update(up_share, up_moment_first[0], up_moment_second[0])
    return (down_update[None], up_update[None], token_loss)


def solution(mesh):
    return jax.shard_map(
        body,
        mesh=mesh,
        in_specs=(
            P(("dp", "owner"), None),
            P(("dp", "owner"), None),
            P(("dp", "owner"), None),
            P("owner", None, "dp"),
            P("owner", None, "dp"),
            P("owner", None, "dp"),
            P("owner", None, "dp"),
            P("owner", None, "dp"),
            P("owner", None, "dp"),
        ),
        out_specs=(P("owner", None, "dp"), P("owner", None, "dp"), P(("dp", "owner"))),
        check_vma=False,
    )
```

profile of v0, /device:TPU:6, one launch (start us, length us, event | category | flops | bytes accessed | tf_op | source)
XLA Modules:
  0.0 467.8 jit_solution(18413843679098739913)
XLA Ops:
  7.9 0.7 fusion.19
  8.8 0.8 select_reduce_fusion
  10.3 2.6 convolution_convert_fusion.1
  12.9 4.9 %reshape.44 = bf16[32,6,8192]{2,1,0:T(8,128)(2,1)} reshape(bf16[192,8192]{1,0:T(8,128)(2,1)} %convolution_convert_fusion.1) | data formatting | bytes 6291456 | tf_op jit(solution)/shard_map/reshape | solution.py:54
  17.8 10.4 %all-to-all-start = ((bf16[32,6,8192]{2,1,0:T(8,128)(2,1)}), bf16[32,6,8192]{2,1,0:T(8,128)(2,1)}, u32[]{:S(2)}, u32[]{:S(2)}) async-start(bf16[32,6,8192]{2,1,0:T(8,128)(2,1)} %reshape.44), calls=%async_computation | async-start | bytes 8388608 | tf_op jit(solution)/shard_map/all_to_all | solution.py:56
  28.3 0.7 all-gather.5.cloned.1.call-update
  29.1 50.0 %all-to-all-done = bf16[32,6,8192]{2,1,0:T(8,128)(2,1)} async-done(((bf16[32,6,8192]{2,1,0:T(8,128)(2,1)}), bf16[32,6,8192]{2,1,0:T(8,128)(2,1)}, u32[]{:S(2)}, u32[]{:S(2)}) %all-to-all-start) | async-done | bytes 3145760 | tf_op jit(solution)/shard_map/all_to_all | solution.py:56
  79.1 4.9 %reshape.45 = bf16[192,8192]{1,0:T(8,128)(2,1)} reshape(bf16[32,6,8192]{2,1,0:T(8,128)(2,1)} %all-to-all-done) | data formatting | bytes 6291456 | tf_op jit(solution)/shard_map/reshape | solution.py:58
  84.0 1.3 all-gather.3.cloned.1.call-done
  85.3 3.3 convolution_convert_fusion.2
  88.6 66.5 %all-gather.5.cloned.1.call-done = bf16[1,64,8192]{2,1,0:T(8,128)(2,1)} async-done(((bf16[1,64,512]{2,1,0:T(8,128)(2,1)}), bf16[1,64,8192]{2,1,0:T(8,128)(2,1)}) %all-gather.5.cloned.1.call-update) | async-done | bytes 1048592 | tf_op jit(solution)/shard_map/all_gather | solution.py:48
  155.0 3.9 fusion
  158.9 4.9 %reshape.46 = bf16[32,6,8192]{2,1,0:T(8,128)(2,1)} reshape(bf16[192,8192]{1,0:T(8,128)(2,1)} %fusion) | data formatting | bytes 6291456 | tf_op jit(solution)/shard_map/reshape | solution.py:67
  163.8 56.6 %all_to_all.15 = bf16[32,6,8192]{2,1,0:T(8,128)(2,1)} all-to-all(bf16[32,6,8192]{2,1,0:T(8,128)(2,1)} %reshape.46), channel_id=1, replica_groups=mesh['dp'=16,'owner'=32] {'owner'}, dimensions={0} | all-to-all | bytes 6291456 | tf_op jit(solution)/shard_map/all_to_all | solution.py:66
  220.4 4.9 %reshape.47 = bf16[192,8192]{1,0:T(8,128)(2,1)} reshape(bf16[32,6,8192]{2,1,0:T(8,128)(2,1)} %all_to_all.15) | data formatting | bytes 6291456 | tf_op jit(solution)/shard_map/reshape | solution.py:73
  225.2 3.9 fusion.1
  229.1 2.6 convolution_convert_fusion
  231.7 4.9 %reshape.48 = bf16[32,6,8192]{2,1,0:T(8,128)(2,1)} reshape(bf16[192,8192]{1,0:T(8,128)(2,1)} %convolution_convert_fusion) | data formatting | bytes 6291456 | tf_op jit(solution)/shard_map/reshape | solution.py:54
  236.6 55.2 %all_to_all.16 = bf16[32,6,8192]{2,1,0:T(8,128)(2,1)} all-to-all(bf16[32,6,8192]{2,1,0:T(8,128)(2,1)} %reshape.48), channel_id=1, replica_groups=mesh['dp'=16,'owner'=32] {'owner'}, dimensions={0} | all-to-all | bytes 6291456 | tf_op jit(solution)/shard_map/all_to_all | solution.py:79
  291.8 4.9 %reshape.49 = bf16[192,8192]{1,0:T(8,128)(2,1)} reshape(bf16[32,6,8192]{2,1,0:T(8,128)(2,1)} %all_to_all.16) | data formatting | bytes 6291456 | tf_op jit(solution)/shard_map/reshape | solution.py:82
  296.7 4.0 convolution_multiply_fusion.1
  300.7 6.5 %fusion.4 = f32[64,8192]{1,0:T(8,128)} fusion(bf16[192,8192]{1,0:T(8,128)(2,1)} %reshape.45, bf16[192,8192]{1,0:T(8,128)(2,1)} %reshape.49, bf16[1,64,8192]{2,1,0:T(8,128)(2,1)S(1)} %copy-done.1), kind=kOutput, calls=%fused_computation.12 | convolution fusion | flops 402677760 | bytes 9437184 | tf_op jit(solution)/shard_map/dot_general | solution.py:95
  307.8 151.6 %all-reduce.3.cloned.1.call-done = (f32[64,8192]{1,0:T(8,128)}, f32[64,8192]{1,0:T(8,128)}) async-done(((f32[64,8192]{1,0:T(8,128)}, f32[64,8192]{1,0:T(8,128)}), (f32[64,8192]{1,0:T(8,128)}, f32[64,8192]{1,0:T(8,128)})) %all-reduce.3.cloned.1.call-update) | async-done | bytes 4194320 | tf_op jit(solution)/shard_map/psum | solution.py:98
  459.4 1.8 fusion.13
  (20 shorter events, 2.2 us)
Async XLA Ops:
  7.2 3.2 copy-start
  7.2 78.1 %all-gather.3.cloned.1.call-start = ((), (), s32[]{:S(2)}) async-start(), calls=%async_computation.3 | async-start | bytes 1114112 | tf_op jit(solution)/shard_map/all_gather | solution.py:47
  17.8 61.2 %all-to-all-start = ((bf16[32,6,8192]{2,1,0:T(8,128)(2,1)}), bf16[32,6,8192]{2,1,0:T(8,128)(2,1)}, u32[]{:S(2)}, u32[]{:S(2)}) async-start(bf16[32,6,8192]{2,1,0:T(8,128)(2,1)} %reshape.44), calls=%async_computation | async-start | bytes 8388608 | tf_op jit(solution)/shard_map/all_to_all | solution.py:56
  28.3 126.8 %all-gather.5.cloned.1.call-start = ((), (), s32[]{:S(2)}) async-start(), calls=%async_computation.4 | async-start | bytes 1114112 | tf_op jit(solution)/shard_map/all_gather | solution.py:48
  29.0 430.4 %all-reduce.3.cloned.1.call-start = ((), (), s32[]{:S(2)}) async-start(), calls=%async_computation.5 | async-start | bytes 8388608 | tf_op jit(solution)/shard_map/psum | solution.py:98
  296.7 4.0 copy-start.1
  307.2 152.2 %copy-start.2 = (bf16[1,64,512]{2,1,0:T(8,128)(2,1)S(1)}, bf16[1,64,512]{2,1,0:T(8,128)(2,1)}, u32[]{:S(2)}) copy-start(bf16[1,64,512]{2,1,0:T(8,128)(2,1)} %param.15) | copy-start | bytes 196612
  307.2 152.2 %copy-start.3 = (bf16[1,64,512]{2,1,0:T(8,128)(2,1)S(1)}, bf16[1,64,512]{2,1,0:T(8,128)(2,1)}, u32[]{:S(2)}) copy-start(bf16[1,64,512]{2,1,0:T(8,128)(2,1)} %param.14) | copy-start | bytes 196612
  307.2 152.2 %copy-start.4 = (bf16[1,64,512]{2,1,0:T(8,128)(2,1)S(1)}, bf16[1,64,512]{2,1,0:T(8,128)(2,1)}, u32[]{:S(2)}) copy-start(bf16[1,64,512]{2,1,0:T(8,128)(2,1)} %param.17) | copy-start | bytes 196612
  307.2 152.2 %copy-start.5 = (bf16[1,64,512]{2,1,0:T(8,128)(2,1)S(1)}, bf16[1,64,512]{2,1,0:T(8,128)(2,1)}, u32[]{:S(2)}) copy-start(bf16[1,64,512]{2,1,0:T(8,128)(2,1)} %param.16) | copy-start | bytes 196612
Sparse Core Ops, SparseCore 0:
  10.1 75.1 all-gather.2
  87.4 67.6 all-gather.4
  307.4 151.9 all-reduce.2
where the time goes:
time: 469 us; the launch traced here: 468 us
  waiting for transfers between devices  271 us (58%)
  blocking collectives  112 us (24%)
  local copies, waits for them, and re-layouts  29.4 us (6%)
  matrix products  26.8 us (6%)
  between operations  13.8 us (3%)
  starting transfers between devices  10.5 us (2%)
  other arithmetic  4.76 us (1%)
    psum x1, waiting for transfers between devices, body(): summed_down, summed_up = lax.psum((down_grad, up_gradient), 'dp')  152 us
    all_gather x1, waiting for transfers between devices, body(): lax.all_gather(adapter_up_weight, 'dp', axis=2, tiled=True)  66.5 us
    all_to_all x1, blocking collectives, body(): lax.all_to_all(adapter_output.reshape(owner_index, slot_capacity, model_w...  56.6 us
    all_to_all x1, blocking collectives, body(): lax.all_to_all(spread(shifted_index.astype(jnp.bfloat16)), 'owner', split...  55.2 us
    all_to_all x1, waiting for transfers between devices, body(): lax.all_to_all(spread(tokens), 'owner', split_axis=0, concat_axis=0, tile...  50 us
    all_to_all x1, starting transfers between devices, body(): lax.all_to_all(spread(tokens), 'owner', split_axis=0, concat_axis=0, tile...  10.4 us
    reshape x2, local copies, waits for them, and re-layouts, spread(): placed_rows(row_block)  9.78 us
  transfers between devices with their start and end apart: 4, of which 4 were waited for; matrix products, arithmetic and copies ran while one was open for 4% of the time, Pallas kernels for 0%

commit v1 on v0

v1 whole, which is shorter than its diff:
```python
import jax
import jax.numpy as jnp
from jax import lax
from jax.sharding import PartitionSpec as P

adapter_scale = 0.5
adam_eps = 1e-08


def adam_update(grad, first, second):
    first_new = 0.9 * first.astype(jnp.float32) + 0.1 * grad
    second_new = 0.95 * second.astype(jnp.float32) + 0.05 * grad * grad
    return first_new / (jnp.sqrt(second_new) + adam_eps)


def body(
    tokens,
    residual,
    token_adapter_index,
    adapter_down_weight,
    adapter_up_weight,
    down_moment_first,
    down_moment_second,
    up_moment_first,
    up_moment_second,
):
    owner_count = lax.axis_size("owner")
    tok_rows = tokens.shape[0]
    width = tokens.shape[1]
    rank = adapter_down_weight.shape[1]
    slot_capacity = max(2, 3 * tok_rows // (2 * owner_count))
    slots = owner_count * slot_capacity
    route_ids = token_adapter_index[:, 0]
    member = (route_ids[:, None] == jnp.arange(owner_count, dtype=jnp.int32)[None, :]).astype(
        jnp.int32
    )
    before = jnp.cumsum(member, axis=0) - member
    within = jnp.sum(before * member, axis=1)
    target = route_ids * slot_capacity + within
    dispatch = (jnp.arange(slots, dtype=jnp.int32)[:, None] == target[None, :]).astype(
        jnp.bfloat16
    )

    both_weights = jnp.concatenate([adapter_down_weight[0], adapter_up_weight[0]], axis=0)
    both_full = lax.all_gather(both_weights, "dp", axis=1, tiled=True)
    down_full = both_full[:rank]
    up_full = both_full[rank:]

    rows = jnp.concatenate([tokens, residual], axis=1)
    placed = jnp.dot(dispatch, rows, preferred_element_type=jnp.float32).astype(jnp.bfloat16)
    arrived_both = lax.all_to_all(
        placed.reshape(owner_count, slot_capacity, 2 * width),
        "owner",
        split_axis=0,
        concat_axis=0,
        tiled=True,
    ).reshape(slots, 2 * width)
    arrived = arrived_both[:, :width]
    arrived_residual = arrived_both[:, width:]

    hidden_state = lax.dot_general(
        arrived, down_full, (((1,), (1,)), ((), ())), preferred_element_type=jnp.float32
    ).astype(jnp.bfloat16)
    adapter_output = (
        adapter_scale * jnp.dot(hidden_state, up_full, preferred_element_type=jnp.float32)
    ).astype(jnp.bfloat16)
    shifted = arrived_residual.astype(jnp.float32) + adapter_output.astype(jnp.float32)
    slot_loss = jnp.mean(0.5 * shifted * shifted, axis=1)
    output_gradient = shifted.astype(jnp.bfloat16)
    up_gradient = adapter_scale * lax.dot_general(
        hidden_state, output_gradient, (((0,), (0,)), ((), ())), preferred_element_type=jnp.float32
    )
    hidden_gradient = (
        adapter_scale
        * lax.dot_general(
            output_gradient,
            up_full,
            (((1,), (1,)), ((), ())),
            preferred_element_type=jnp.float32,
        )
    ).astype(jnp.bfloat16)
    down_grad = lax.dot_general(
        hidden_gradient, arrived, (((0,), (0,)), ((), ())), preferred_element_type=jnp.float32
    )

    both_grads = jnp.concatenate([down_grad, up_gradient], axis=0)
    summed = lax.psum_scatter(both_grads, "dp", scatter_dimension=1, tiled=True)
    down_share = summed[:rank]
    up_share = summed[rank:]
    down_update = adam_update(down_share, down_moment_first[0], down_moment_second[0])
    up_update = adam_update(up_share, up_moment_first[0], up_moment_second[0])

    returned_loss = lax.all_to_all(
        slot_loss.reshape(owner_count, slot_capacity),
        "owner",
        split_axis=0,
        concat_axis=0,
        tiled=True,
    ).reshape(slots)
    token_loss = jnp.take(returned_loss, target, axis=0)
    return (down_update[None], up_update[None], token_loss)


def solution(mesh):
    return jax.shard_map(
        body,
        mesh=mesh,
        in_specs=(
            P(("dp", "owner"), None),
            P(("dp", "owner"), None),
            P(("dp", "owner"), None),
            P("owner", None, "dp"),
            P("owner", None, "dp"),
            P("owner", None, "dp"),
            P("owner", None, "dp"),
            P("owner", None, "dp"),
            P("owner", None, "dp"),
        ),
        out_specs=(P("owner", None, "dp"), P("owner", None, "dp"), P(("dp", "owner"))),
        check_vma=False,
    )
```

time: 469 us -> 277 us (0.59)
  blocking collectives: 112 us -> 0 us
  waiting for transfers between devices: 271 us -> 169 us
  starting transfers between devices: 10.5 us -> 38.8 us
  local copies, waits for them, and re-layouts: 29.4 us -> 21.3 us
  other arithmetic: 4.76 us -> 10.7 us
  matrix products: 26.8 us -> 21.5 us
    psum x1 -> x0, waiting for transfers between devices: 152 us -> none  [body(): summed_down, summed_up = lax.psum((down_grad, up_gradient), 'dp')]
    all_to_all x2 -> x0, blocking collectives: 112 us -> none  [the longest x1 56.6 us: body(): lax.all_to_all(adapter_output.reshape(owner_index, slot_capacity, model_w...]
    all_gather x2 -> x1, waiting for transfers between devices: 67.7 us -> 0.01 us  [body(): both_full = lax.all_gather(both_weights, 'dp', axis=1, tiled=True)]
    reduce_scatter x0 -> x1, waiting for transfers between devices: none -> 60.8 us  [body(): summed = lax.psum_scatter(both_grads, 'dp', scatter_dimension=1, tiled=True)]
    all_to_all x1 -> x2, waiting for transfers between devices: 50 us -> 108 us  [the longest x1 103 us: body(): lax.all_to_all(placed.reshape(owner_count, slot_capacity, 2 * width), 'ow...]
    all_to_all x1 -> x2, starting transfers between devices: 10.4 us -> 38.7 us  [the longest x1 28.1 us: body(): lax.all_to_all(slot_loss.reshape(owner_count, slot_capacity), 'owner', sp...]
    reshape x6 -> x3, local copies, waits for them, and re-layouts: 29.4 us -> 18.2 us  [the longest x1 9.1 us: body(): arrived_both = lax.all_to_all(placed.reshape(owner_count, slot_capacity,...]
    concatenate x0 -> x2, other arithmetic: none -> 5.22 us  [the longest x1 4.56 us: body(): both_grads = jnp.concatenate([down_grad, up_gradient], axis=0)]
  transfers between devices with their start and end apart: 4 -> 4, of which waited for: 4 -> 3; matrix products, arithmetic and copies ran while one was open for 4% -> 5% of each run, Pallas kernels for 0% -> 0%
where the time goes in v1:
time: 277 us; the launch traced here: 276 us
  waiting for transfers between devices  169 us (61%)
  starting transfers between devices  38.8 us (14%)
  matrix products  21.5 us (8%)
  local copies, waits for them, and re-layouts  21.3 us (8%)
  between operations  14.2 us (5%)
  other arithmetic  10.7 us (4%)
    all_to_all x1, waiting for transfers between devices, body(): lax.all_to_all(placed.reshape(owner_count, slot_capacity, 2 * width), 'ow...  103 us
    reduce_scatter x1, waiting for transfers between devices, body(): summed = lax.psum_scatter(both_grads, 'dp', scatter_dimension=1, tiled=True)  60.8 us
    all_to_all x1, starting transfers between devices, body(): lax.all_to_all(slot_loss.reshape(owner_count, slot_capacity), 'owner', sp...  28.1 us
    all_to_all x1, starting transfers between devices, body(): lax.all_to_all(placed.reshape(owner_count, slot_capacity, 2 * width), 'ow...  10.7 us
    reshape x1, local copies, waits for them, and re-layouts, body(): arrived_both = lax.all_to_all(placed.reshape(owner_count, slot_capacity,...  9.1 us
    reshape x1, local copies, waits for them, and re-layouts, body(): placed.reshape(owner_count, slot_capacity, 2 * width)  8.97 us
    dot_general x1, matrix products, body(): jnp.dot(dispatch, rows, preferred_element_type=jnp.float32)  6.65 us
    dot_general x1, matrix products, body(): lax.dot_general(hidden_gradient, arrived, (((0,), (0,)), ((), ())), prefe...  5.9 us
  transfers between devices with their start and end apart: 4, of which 3 were waited for; matrix products, arithmetic and copies ran while one was open for 5% of the time, Pallas kernels for 0%

profile of v1, /device:TPU:6, one launch (start us, length us, event | category | flops | bytes accessed | tf_op | source)
XLA Modules:
  0.0 275.7 jit_solution(10029577470650876318)
XLA Ops:
  7.2 0.7 fusion.39
  8.1 0.8 select_reduce_fusion
  8.9 0.7 multiply_add_fusion
  9.6 6.7 %convolution_convert_fusion = bf16[192,16384]{1,0:T(8,128)(2,1)} fusion(bf16[128,8192]{1,0:T(8,128)(2,1)} %param.10, bf16[128,8192]{1,0:T(8,128)(2,1)} %param.9, s32[128]{0:T(128)S(1)} %multiply_add_fusion), kind=kOutput, calls=%fused_computation.1 | convolution fusion | flops 816865280 | bytes 10486272 | tf_op jit(solution)/shard_map/dot_general | solution.py:50
  16.2 9.0 %reshape.58 = bf16[32,6,16384]{2,1,0:T(8,128)(2,1)} reshape(bf16[192,16384]{1,0:T(8,128)(2,1)} %convolution_convert_fusion) | data formatting | bytes 12582912 | tf_op jit(solution)/shard_map/reshape | solution.py:52
  25.2 10.7 %all-to-all-start = ((bf16[32,6,16384]{2,1,0:T(8,128)(2,1)}), bf16[32,6,16384]{2,1,0:T(8,128)(2,1)}, u32[]{:S(2)}, u32[]{:S(2)}) async-start(bf16[32,6,16384]{2,1,0:T(8,128)(2,1)} %reshape.58), calls=%async_computation | async-start | bytes 16777216 | tf_op jit(solution)/shard_map/all_to_all | solution.py:51
  35.9 0.7 pad_maximum_fusion.1
  36.7 102.9 %all-to-all-done = bf16[32,6,16384]{2,1,0:T(8,128)(2,1)} async-done(((bf16[32,6,16384]{2,1,0:T(8,128)(2,1)}), bf16[32,6,16384]{2,1,0:T(8,128)(2,1)}, u32[]{:S(2)}, u32[]{:S(2)}) %all-to-all-start) | async-done | bytes 6291488 | tf_op jit(solution)/shard_map/all_to_all | solution.py:51
  139.6 9.1 %reshape.59 = bf16[192,16384]{1,0:T(8,128)(2,1)} reshape(bf16[32,6,16384]{2,1,0:T(8,128)(2,1)} %all-to-all-done) | data formatting | bytes 12582912 | tf_op jit(solution)/shard_map/reshape | solution.py:57
  148.7 3.4 %fusion.20 = bf16[192,64]{0,1:T(8,128)(2,1)S(1)} fusion(bf16[192,16384]{1,0:T(8,128)(2,1)} %reshape.59, bf16[128,8192]{1,0:T(8,128)(2,1)} %all-gather.2.cloned.1.call-done), kind=kOutput, calls=%fused_computation.22 | convolution fusion | flops 201338880 | bytes 4218880 | tf_op jit(solution)/shard_map/dot_general | solution.py:61
  152.2 3.5 %fusion.3 = (f32[192]{0:T(256)S(1)}, bf16[192,8192]{1,0:T(8,128)(2,1)S(1)}) fusion(bf16[192,64]{0,1:T(8,128)(2,1)S(1)} %fusion.20, bf16[128,8192]{1,0:T(8,128)(2,1)S(1)} %copy-done, bf16[192,16384]{1,0:T(8,128)(2,1)} %reshape.59), kind=kOutput, calls=%fused_computation.8 | convolution fusion | flops 215482176 | bytes 7373568 | tf_op jit(solution)/shard_map/dot_general | solution.py:65
  155.7 2.0 convolution_multiply_fusion.1
  157.7 5.9 %fusion.7 = f32[64,8192]{1,0:T(8,128)} fusion(bf16[192,16384]{1,0:T(8,128)(2,1)} %reshape.59, bf16[192,8192]{1,0:T(8,128)(2,1)S(1)} %get-tuple-element.6, bf16[128,8192]{1,0:T(8,128)(2,1)} %all-gather.2.cloned.1.call-done), kind=kOutput, calls=%fused_computation.13 | convolution fusion | flops 402677760 | bytes 9437184 | tf_op jit(solution)/shard_map/dot_general | solution.py:82
  163.6 4.6 %pad_maximum_fusion = f32[128,8192]{1,0:T(8,128)} fusion(f32[64,8192]{1,0:T(8,128)} %convolution_multiply_fusion.1, f32[64,8192]{1,0:T(8,128)} %fusion.7), kind=kLoop, calls=%fused_computation.12 | loop fusion | flops 1048576 | bytes 8388608 | tf_op jit(solution)/shard_map/concatenate | solution.py:86
  168.2 0.6 copy-done.7
  168.8 0.7 div.18
  169.6 28.1 %all-to-all-start.1 = ((f32[32,1,6]{2,1,0:T(1,128)}), f32[32,1,6]{2,1,0:T(1,128)S(1)}, u32[]{:S(2)}, u32[]{:S(2)}) async-start(f32[32,1,6]{2,1,0:T(1,128)} %bitcast.11), calls=%async_computation.2 | async-start | bytes 32768 | tf_op jit(solution)/shard_map/all_to_all | solution.py:93
  197.6 5.4 %all-to-all-done.1 = f32[32,1,6]{2,1,0:T(1,128)S(1)} async-done(((f32[32,1,6]{2,1,0:T(1,128)}), f32[32,1,6]{2,1,0:T(1,128)S(1)}, u32[]{:S(2)}, u32[]{:S(2)}) %all-to-all-start.1) | async-done | bytes 800 | tf_op jit(solution)/shard_map/all_to_all | solution.py:93
  203.0 0.5 broadcast.79
  203.6 0.7 reduce.3
  204.4 1.3 gather_fusion
  205.6 0.5 bitcast_select_fusion
  206.1 60.8 %reduce-scatter.2.cloned.1.call-done = f32[128,512]{1,0:T(8,128)} async-done(((f32[128,8192]{1,0:T(8,128)}), f32[128,512]{1,0:T(8,128)}) %reduce-scatter.2.cloned.1.call-update) | async-done | bytes 262160 | tf_op jit(solution)/shard_map/reduce_scatter | solution.py:87
  267.0 1.8 fusion.38
  (25 shorter events, 0.4 us)
Async XLA Ops:
  25.2 10.7 %copy-start.5 = (bf16[1,64,512]{2,1,0:T(8,128)(2,1)S(1)}, bf16[1,64,512]{2,1,0:T(8,128)(2,1)}, u32[]{:S(2)}) copy-start(bf16[1,64,512]{2,1,0:T(8,128)(2,1)} %param.13) | copy-start | bytes 196612
  25.2 10.7 %copy-start.6 = (bf16[1,64,512]{2,1,0:T(8,128)(2,1)S(1)}, bf16[1,64,512]{2,1,0:T(8,128)(2,1)}, u32[]{:S(2)}) copy-start(bf16[1,64,512]{2,1,0:T(8,128)(2,1)} %param.12) | copy-start | bytes 196612
  25.2 114.4 %all-to-all-start = ((bf16[32,6,16384]{2,1,0:T(8,128)(2,1)}), bf16[32,6,16384]{2,1,0:T(8,128)(2,1)}, u32[]{:S(2)}, u32[]{:S(2)}) async-start(bf16[32,6,16384]{2,1,0:T(8,128)(2,1)} %reshape.58), calls=%async_computation | async-start | bytes 16777216 | tf_op jit(solution)/shard_map/all_to_all | solution.py:51
  35.9 112.8 %all-gather.2.cloned.1.call-start = ((), (), s32[]{:S(2)}) async-start(), calls=%async_computation.3 | async-start | bytes 2228224 | tf_op jit(solution)/shard_map/all_gather | solution.py:45
  36.6 230.3 %reduce-scatter.2.cloned.1.call-start = ((), (), s32[]{:S(2)}) async-start(), calls=%async_computation.4 | async-start | bytes 4456448 | tf_op jit(solution)/shard_map/reduce_scatter | solution.py:87
  148.7 3.4 %copy-start = (bf16[128,8192]{1,0:T(8,128)(2,1)S(1)}, bf16[128,8192]{1,0:T(8,128)(2,1)}, u32[]{:S(2)}) copy-start(bf16[128,8192]{1,0:T(8,128)(2,1)} %all-gather.2.cloned.1.call-done) | copy-start | bytes 6291460
  168.2 0.7 copy-start.7
  168.2 98.8 %copy-start.1 = (bf16[1,64,512]{2,1,0:T(8,128)(2,1)S(1)}, bf16[1,64,512]{2,1,0:T(8,128)(2,1)}, u32[]{:S(2)}) copy-start(bf16[1,64,512]{2,1,0:T(8,128)(2,1)} %param.17) | copy-start | bytes 196612
  168.2 98.8 %copy-start.2 = (bf16[1,64,512]{2,1,0:T(8,128)(2,1)S(1)}, bf16[1,64,512]{2,1,0:T(8,128)(2,1)}, u32[]{:S(2)}) copy-start(bf16[1,64,512]{2,1,0:T(8,128)(2,1)} %param.16) | copy-start | bytes 196612
  168.2 98.8 %copy-start.3 = (bf16[1,64,512]{2,1,0:T(8,128)(2,1)S(1)}, bf16[1,64,512]{2,1,0:T(8,128)(2,1)}, u32[]{:S(2)}) copy-start(bf16[1,64,512]{2,1,0:T(8,128)(2,1)} %param.15) | copy-start | bytes 196612
  168.2 98.8 %copy-start.4 = (bf16[1,64,512]{2,1,0:T(8,128)(2,1)S(1)}, bf16[1,64,512]{2,1,0:T(8,128)(2,1)}, u32[]{:S(2)}) copy-start(bf16[1,64,512]{2,1,0:T(8,128)(2,1)} %param.14) | copy-start | bytes 196612
  169.6 33.5 %all-to-all-start.1 = ((f32[32,1,6]{2,1,0:T(1,128)}), f32[32,1,6]{2,1,0:T(1,128)S(1)}, u32[]{:S(2)}, u32[]{:S(2)}) async-start(f32[32,1,6]{2,1,0:T(1,128)} %bitcast.11), calls=%async_computation.2 | async-start | bytes 32768 | tf_op jit(solution)/shard_map/all_to_all | solution.py:93
Sparse Core Ops, SparseCore 0:
  39.3 74.0 all-gather.1
  168.3 98.5 reduce-scatter.1

commit v2 on v1

--- a/solution.py
+++ b/solution.py
@@ -41,50 +41,50 @@
         jnp.bfloat16
     )
 
+    pieces = lax.axis_size("dp")
+    piece = width // pieces
+    valid = jnp.sum(dispatch, axis=1) > 0
+    source = jnp.argmax(dispatch, axis=1)
+
     both_weights = jnp.concatenate([adapter_down_weight[0], adapter_up_weight[0]], axis=0)
-    both_full = lax.all_gather(both_weights, "dp", axis=1, tiled=True)
-    down_full = both_full[:rank]
-    up_full = both_full[rank:]
+    both_split = lax.all_gather(both_weights, "dp", axis=0, tiled=False)
+    down_full = both_split[:, :rank]
+    up_full = both_split[:, rank:]
 
-    rows = jnp.concatenate([tokens, residual], axis=1)
-    placed = jnp.dot(dispatch, rows, preferred_element_type=jnp.float32).astype(jnp.bfloat16)
-    arrived_both = lax.all_to_all(
-        placed.reshape(owner_count, slot_capacity, 2 * width),
-        "owner",
-        split_axis=0,
-        concat_axis=0,
-        tiled=True,
-    ).reshape(slots, 2 * width)
-    arrived = arrived_both[:, :width]
-    arrived_residual = arrived_both[:, width:]
+    def place(row_block):
+        split_rows = row_block.reshape(tok_rows, pieces, piece)
+        picked = jnp.where(valid[:, None, None], split_rows[source], jnp.zeros((), row_block.dtype))
+        return picked.reshape(owner_count, slot_capacity * pieces, piece)
 
-    hidden_state = lax.dot_general(
-        arrived, down_full, (((1,), (1,)), ((), ())), preferred_element_type=jnp.float32
+    placed = jnp.concatenate([place(tokens), place(residual)], axis=1)
+    arrived_both = lax.all_to_all(placed, "owner", split_axis=0, concat_axis=0, tiled=True)
+    half = slot_capacity * pieces
+    arrived = arrived_both[:, :half].reshape(slots, pieces, piece)
+    arrived_residual = arrived_both[:, half:].reshape(slots, pieces, piece)
+
+    hidden_state = jnp.einsum(
+        "tkc,krc->tr", arrived, down_full, preferred_element_type=jnp.float32
     ).astype(jnp.bfloat16)
     adapter_output = (
-        adapter_scale * jnp.dot(hidden_state, up_full, preferred_element_type=jnp.float32)
+        adapter_scale
+        * jnp.einsum("tr,krc->tkc", hidden_state, up_full, preferred_element_type=jnp.float32)
     ).astype(jnp.bfloat16)
     shifted = arrived_residual.astype(jnp.float32) + adapter_output.astype(jnp.float32)
-    slot_loss = jnp.mean(0.5 * shifted * shifted, axis=1)
+    slot_loss = jnp.mean(0.5 * shifted * shifted, axis=(1, 2))
     output_gradient = shifted.astype(jnp.bfloat16)
-    up_gradient = adapter_scale * lax.dot_general(
-        hidden_state, output_gradient, (((0,), (0,)), ((), ())), preferred_element_type=jnp.float32
+    up_gradient = adapter_scale * jnp.einsum(
+        "tr,tkc->krc", hidden_state, output_gradient, preferred_element_type=jnp.float32
     )
     hidden_gradient = (
         adapter_scale
-        * lax.dot_general(
-            output_gradient,
-            up_full,
-            (((1,), (1,)), ((), ())),
-            preferred_element_type=jnp.float32,
-        )
+        * jnp.einsum("tkc,krc->tr", output_gradient, up_full, preferred_element_type=jnp.float32)
     ).astype(jnp.bfloat16)
-    down_grad = lax.dot_general(
-        hidden_gradient, arrived, (((0,), (0,)), ((), ())), preferred_element_type=jnp.float32
+    down_grad = jnp.einsum(
+        "tr,tkc->krc", hidden_gradient, arrived, preferred_element_type=jnp.float32
     )
 
-    both_grads = jnp.concatenate([down_grad, up_gradient], axis=0)
-    summed = lax.psum_scatter(both_grads, "dp", scatter_dimension=1, tiled=True)
+    both_grads = jnp.concatenate([down_grad, up_gradient], axis=1)
+    summed = lax.psum_scatter(both_grads, "dp", scatter_dimension=0, tiled=False)
     down_share = summed[:rank]
     up_share = summed[rank:]
     down_update = adam_update(down_share, down_moment_first[0], down_moment_second[0])

time: 277 us -> 259 us (0.935)
  waiting for transfers between devices: 169 us -> 148 us
  starting transfers between devices: 38.8 us -> 24.9 us
  matrix products: 21.5 us -> 34.1 us
  other arithmetic: 10.7 us -> 19.5 us
  local copies, waits for them, and re-layouts: 21.3 us -> 18.4 us
    all_to_all x1, waiting for transfers between devices: 103 us -> 76.2 us  [body(): lax.all_to_all(placed, 'owner', split_axis=0, concat_axis=0, tiled=True)]
    reshape x2 -> x0, local copies, waits for them, and re-layouts: 18.1 us -> none  [the longest x1 9.1 us: body(): arrived_both = lax.all_to_all(placed.reshape(owner_count, slot_capacity,...]
    all_to_all x1, starting transfers between devices: 28.1 us -> 14 us  [body(): lax.all_to_all(slot_loss.reshape(owner_count, slot_capacity), 'owner', sp...]
    dot_general x5 -> x4, matrix products: 21.5 us -> 34.1 us  [the longest x1 12.3 us: body(): jnp.einsum('tr,tkc->krc', hidden_gradient, arrived, preferred_element_typ...]
    gather x0 -> x2, local copies, waits for them, and re-layouts: none -> 6.94 us  [place(): split_rows[source]]
    reduce_scatter x1, waiting for transfers between devices: 60.8 us -> 65.9 us  [body(): lax.psum_scatter(both_grads, 'dp', scatter_dimension=0, tiled=False)]
    unnamed x16 -> x22, local copies, waits for them, and re-layouts: 0.63 us -> 5.27 us
    convert_element_type x0 -> x1, other arithmetic: none -> 3.56 us  [body(): arrived_residual.astype(jnp.float32) + adapter_output.astype(jnp.float32)]
  transfers between devices with their start and end apart: 4 -> 4, of which waited for: 3 -> 3; matrix products, arithmetic and copies ran while one was open for 5% -> 4% of each run, Pallas kernels for 0% -> 0%
where the time goes in v2:
time: 259 us
  waiting for transfers between devices  148 us (57%)
  matrix products  34.1 us (13%)
  starting transfers between devices  24.9 us (10%)
  other arithmetic  19.5 us (8%)
  local copies, waits for them, and re-layouts  18.4 us (7%)
  between operations  14.2 us (5%)
    all_to_all x1, waiting for transfers between devices, body(): lax.all_to_all(placed, 'owner', split_axis=0, concat_axis=0, tiled=True)  76.2 us
    reduce_scatter x1, waiting for transfers between devices, body(): lax.psum_scatter(both_grads, 'dp', scatter_dimension=0, tiled=False)  65.9 us
    all_to_all x1, starting transfers between devices, body(): lax.all_to_all(slot_loss.reshape(owner_count, slot_capacity), 'owner', sp...  14 us
    dot_general x1, matrix products, body(): jnp.einsum('tr,tkc->krc', hidden_gradient, arrived, preferred_element_typ...  12.3 us
    all_to_all x1, starting transfers between devices, body(): lax.all_to_all(placed, 'owner', split_axis=0, concat_axis=0, tiled=True)  10.6 us
    dot_general x1, matrix products, body(): jnp.einsum('tr,krc->tkc', hidden_state, up_full, preferred_element_type=j...  9.31 us
    dot_general x1, matrix products, body(): jnp.einsum('tr,tkc->krc', hidden_state, output_gradient, preferred_elemen...  7.63 us
    gather x2, local copies, waits for them, and re-layouts, place(): split_rows[source]  6.94 us
  transfers between devices with their start and end apart: 4, of which 3 were waited for; matrix products, arithmetic and copies ran while one was open for 4% of the time, Pallas kernels for 0%

profile of v2, /device:TPU:6, one launch (start us, length us, event | category | flops | bytes accessed | tf_op | source)
XLA Modules:
  0.0 258.6 jit_solution(7004991521548012042)
XLA Ops:
  7.2 0.7 fusion.36
  8.1 1.0 select_reduce_fusion
  10.5 3.8 %copy.30 = bf16[16,8,16,512]{3,2,1,0:T(8,128)(2,1)} copy(bf16[16,8,16,512]{3,1,2,0:T(8,128)(2,1)} %bitcast.61) | data formatting | bytes 4194304
  14.3 0.8 copy.29
  15.1 4.2 %gather_fusion.1 = bf16[192,16,512]{2,1,0:T(8,128)(2,1)} fusion(bf16[128,16,512]{2,1,0:T(8,128)(2,1)} %bitcast.55, s32[1024]{0:T(1024)S(1)} %pad_clamp_fusion.1), kind=kCustom, calls=%fused_computation.1 | custom fusion | bytes 6292224 | tf_op jit(solution)/shard_map/gather | solution.py:56
  19.4 2.7 %gather_fusion = bf16[192,16,512]{2,1,0:T(8,128)(2,1)} fusion(bf16[128,16,512]{2,1,0:T(8,128)(2,1)S(1)} %bitcast.54, s32[1024]{0:T(1024)S(1)} %pad_clamp_fusion.1), kind=kCustom, calls=%fused_computation | custom fusion | bytes 6292224 | tf_op jit(solution)/shard_map/gather | solution.py:56
  22.4 3.2 %bitcast_select_fusion.1 = (bf16[32,96,512]{2,1,0:T(8,128)(2,1)S(1)}, bf16[32,96,512]{2,1,0:T(8,128)(2,1)S(1)}) fusion(pred[32,96]{1,0:T(8,128)(4,1)S(1)} %copy.24, bf16[32,96,512]{2,1,0:T(8,128)(2,1)} %bitcast.57, bf16[32,96,512]{2,1,0:T(8,128)(2,1)} %bitcast.56), kind=kLoop, calls=%fused_computation.11 | loop fusion | flops 3145728 | bytes 12585984 | tf_op jit(solution)/shard_map/jit(_where)/select_n | solution.py:56
  25.6 3.3 %pad_maximum_fusion = bf16[32,192,512]{2,1,0:T(8,128)(2,1)} fusion(bf16[32,96,512]{2,1,0:T(8,128)(2,1)S(1)} %get-tuple-element.10, bf16[32,96,512]{2,1,0:T(8,128)(2,1)S(1)} %get-tuple-element.9), kind=kLoop, calls=%fused_computation.5 | loop fusion | flops 12582912 | bytes 12582912 | tf_op jit(solution)/shard_map/concatenate | solution.py:59
  28.9 10.6 %all-to-all-start = ((bf16[32,192,512]{2,1,0:T(8,128)(2,1)}), bf16[32,192,512]{2,1,0:T(8,128)(2,1)}, u32[]{:S(2)}, u32[]{:S(2)}) async-start(bf16[32,192,512]{2,1,0:T(8,128)(2,1)} %pad_maximum_fusion), calls=%async_computation | async-start | bytes 12582912 | tf_op jit(solution)/shard_map/all_to_all | solution.py:60
  40.5 76.2 %all-to-all-done = bf16[32,192,512]{2,1,0:T(8,128)(2,1)} async-done(((bf16[32,192,512]{2,1,0:T(8,128)(2,1)}), bf16[32,192,512]{2,1,0:T(8,128)(2,1)}, u32[]{:S(2)}, u32[]{:S(2)}) %all-to-all-start) | async-done | bytes 6291488 | tf_op jit(solution)/shard_map/all_to_all | solution.py:60
  116.7 3.3 %fusion.42 = (bf16[32,96,512]{2,1,0:T(8,128)(2,1)S(1)}, bf16[32,96,512]{2,1,0:T(8,128)(2,1)S(1)}) fusion(bf16[32,192,512]{2,1,0:T(8,128)(2,1)} %all-to-all-done), kind=kLoop, calls=%fused_computation.57 | loop fusion | bytes 12582912 | tf_op jit(solution)/shard_map/slice | solution.py:63
  120.0 3.6 %convert.2 = f32[192,16,512]{2,1,0:T(8,128)} convert(bf16[192,16,512]{2,1,0:T(8,128)(2,1)S(1)} %bitcast.58) | non-fusion elementwise | flops 1572864 | bytes 9437184 | tf_op jit(solution)/shard_map/convert_element_type | solution.py:72
  123.5 4.8 %fusion.17 = bf16[192,64,1]{0,1,2:T(8,128)(2,1)S(1)} fusion(bf16[192,16,512]{2,1,0:T(8,128)(2,1)S(1)} %bitcast.59, bf16[16,128,512]{2,1,0:T(8,128)(2,1)} %bitcast.63), kind=kOutput, calls=%fused_computation.23 | convolution fusion | flops 201338880 | bytes 4218880 | tf_op jit(solution)/shard_map/tkc,krc->tr/dot_general | solution.py:65
  128.4 9.3 %fusion = (f32[192]{0:T(256)S(1)}, bf16[192,16,512]{2,0,1:T(8,128)(2,1)}) fusion(f32[192,16,512]{2,1,0:T(8,128)} %convert.2, bf16[192,64,1]{0,1,2:T(8,128)(2,1)S(1)} %fusion.17, bf16[16,128,512]{2,1,0:T(8,128)(2,1)S(1)} %bitcast.65), kind=kOutput, calls=%fused_computation.4 | convolution fusion | flops 212336448 | bytes 10519296 | tf_op jit(solution)/shard_map/tr,krc->tkc/dot_general | solution.py:70
  137.7 12.3 %fusion.6 = f32[16,64,512]{2,1,0:T(8,128)} fusion(bf16[192,16,512]{2,1,0:T(8,128)(2,1)S(1)} %bitcast.60, bf16[16,128,512]{2,1,0:T(8,128)(2,1)} %bitcast.64, bf16[192,16,512]{2,0,1:T(8,128)(2,1)} %get-tuple-element.12, f32[192,16,512]{2,1,0:T(8,128)} %convert.2), kind=kOutput, calls=%fused_computation.17 | convolution fusion | flops 407396352 | bytes 15728640 | tf_op jit(solution)/shard_map/tr,tkc->krc/dot_general | solution.py:82
  150.0 7.6 %multiply_bitcast_fusion = f32[16,64,512]{2,1,0:T(8,128)S(1)} fusion(bf16[192,64,1]{0,1,2:T(8,128)(2,1)S(1)} %fusion.17, bf16[192,16,512]{2,0,1:T(8,128)(2,1)} %get-tuple-element.12, f32[192,16,512]{2,1,0:T(8,128)} %convert.2), kind=kOutput, calls=%fused_computation.16 | convolution fusion | flops 206569472 | bytes 11558912 | tf_op jit(solution)/shard_map/tr,tkc->krc/dot_general | solution.py:75
  157.7 2.4 pad_maximum_fusion.1
  160.7 0.7 div.20
  161.4 14.0 %all-to-all-start.1 = ((f32[32,1,6]{2,1,0:T(1,128)}), f32[32,1,6]{2,1,0:T(1,128)S(1)}, u32[]{:S(2)}, u32[]{:S(2)}) async-start(f32[32,1,6]{2,1,0:T(1,128)} %bitcast.17), calls=%async_computation.2 | async-start | bytes 32768 | tf_op jit(solution)/shard_map/all_to_all | solution.py:93
  175.5 5.4 %all-to-all-done.1 = f32[32,1,6]{2,1,0:T(1,128)S(1)} async-done(((f32[32,1,6]{2,1,0:T(1,128)}), f32[32,1,6]{2,1,0:T(1,128)S(1)}, u32[]{:S(2)}, u32[]{:S(2)}) %all-to-all-start.1) | async-done | bytes 800 | tf_op jit(solution)/shard_map/all_to_all | solution.py:93
  181.4 0.7 reduce.23
  182.2 1.3 gather_fusion.2
  184.0 65.9 %reduce-scatter.2.cloned.1.call-done = f32[1,128,512]{2,1,0:T(8,128)} async-done(((f32[16,128,512]{2,1,0:T(8,128)}), f32[1,128,512]{2,1,0:T(8,128)}) %reduce-scatter.2.cloned.1.call-update) | async-done | bytes 262160 | tf_op jit(solution)/shard_map/reduce_scatter | solution.py:87
  249.9 1.8 fusion.33
  (43 shorter events, 4.6 us)
Async XLA Ops:
  8.1 6.2 %copy-start.1 = (bf16[128,8192]{1,0:T(8,128)(2,1)S(1)}, bf16[128,8192]{1,0:T(8,128)(2,1)}, u32[]{:S(2)}) copy-start(bf16[128,8192]{1,0:T(8,128)(2,1)} %param.9) | copy-start | bytes 6291460
  28.9 10.7 %copy-start.7 = (bf16[1,64,512]{2,1,0:T(8,128)(2,1)S(1)}, bf16[1,64,512]{2,1,0:T(8,128)(2,1)}, u32[]{:S(2)}) copy-start(bf16[1,64,512]{2,1,0:T(8,128)(2,1)} %param.13) | copy-start | bytes 196612
  28.9 10.7 %copy-start.8 = (bf16[1,64,512]{2,1,0:T(8,128)(2,1)S(1)}, bf16[1,64,512]{2,1,0:T(8,128)(2,1)}, u32[]{:S(2)}) copy-start(bf16[1,64,512]{2,1,0:T(8,128)(2,1)} %param.12) | copy-start | bytes 196612
  28.9 87.7 %all-to-all-start = ((bf16[32,192,512]{2,1,0:T(8,128)(2,1)}), bf16[32,192,512]{2,1,0:T(8,128)(2,1)}, u32[]{:S(2)}, u32[]{:S(2)}) async-start(bf16[32,192,512]{2,1,0:T(8,128)(2,1)} %pad_maximum_fusion), calls=%async_computation | async-start | bytes 12582912 | tf_op jit(solution)/shard_map/all_to_all | solution.py:60
  39.5 84.0 %all-gather.3.cloned.1.call-start = ((), (), s32[]{:S(2)}) async-start(), calls=%async_computation.4 | async-start | bytes 2228224 | tf_op jit(solution)/shard_map/all_gather | solution.py:50
  40.3 209.6 %reduce-scatter.2.cloned.1.call-start = ((), (), s32[]{:S(2)}) async-start(), calls=%async_computation.3 | async-start | bytes 4456448 | tf_op jit(solution)/shard_map/reduce_scatter | solution.py:87
  123.5 4.8 %copy-start.2 = (bf16[2048,512]{1,0:T(8,128)(2,1)S(1)}, bf16[2048,512]{1,0:T(8,128)(2,1)}, u32[]{:S(2)}) copy-start(bf16[2048,512]{1,0:T(8,128)(2,1)} %all-gather.3.cloned.1.call-done) | copy-start | bytes 6291460
  150.0 7.6 %copy-start = (f32[16,64,512]{2,1,0:T(8,128)S(1)}, f32[16,64,512]{2,1,0:T(8,128)}, u32[]{:S(2)}) copy-start(f32[16,64,512]{2,1,0:T(8,128)} %fusion.6) | copy-start | bytes 6291460
  160.1 0.7 copy-start.9
  160.1 89.9 %copy-start.3 = (bf16[1,64,512]{2,1,0:T(8,128)(2,1)S(1)}, bf16[1,64,512]{2,1,0:T(8,128)(2,1)}, u32[]{:S(2)}) copy-start(bf16[1,64,512]{2,1,0:T(8,128)(2,1)} %param.17) | copy-start | bytes 196612
  160.1 89.9 %copy-start.4 = (bf16[1,64,512]{2,1,0:T(8,128)(2,1)S(1)}, bf16[1,64,512]{2,1,0:T(8,128)(2,1)}, u32[]{:S(2)}) copy-start(bf16[1,64,512]{2,1,0:T(8,128)(2,1)} %param.16) | copy-start | bytes 196612
  160.1 89.9 %copy-start.5 = (bf16[1,64,512]{2,1,0:T(8,128)(2,1)S(1)}, bf16[1,64,512]{2,1,0:T(8,128)(2,1)}, u32[]{:S(2)}) copy-start(bf16[1,64,512]{2,1,0:T(8,128)(2,1)} %param.15) | copy-start | bytes 196612
  160.1 89.9 %copy-start.6 = (bf16[1,64,512]{2,1,0:T(8,128)(2,1)S(1)}, bf16[1,64,512]{2,1,0:T(8,128)(2,1)}, u32[]{:S(2)}) copy-start(bf16[1,64,512]{2,1,0:T(8,128)(2,1)} %param.14) | copy-start | bytes 196612
  161.4 19.4 %all-to-all-start.1 = ((f32[32,1,6]{2,1,0:T(1,128)}), f32[32,1,6]{2,1,0:T(1,128)S(1)}, u32[]{:S(2)}, u32[]{:S(2)}) async-start(f32[32,1,6]{2,1,0:T(1,128)} %bitcast.17), calls=%async_computation.2 | async-start | bytes 32768 | tf_op jit(solution)/shard_map/all_to_all | solution.py:93
Sparse Core Ops, SparseCore 0:
  43.0 73.9 all-gather.2
  160.2 89.6 reduce-scatter.1

commit v3 on v1

--- a/solution.py
+++ b/solution.py
@@ -41,22 +41,26 @@
         jnp.bfloat16
     )
 
+    pieces = lax.axis_size("dp")
+    piece = width // pieces
+    valid = jnp.sum(dispatch, axis=1) > 0
+    source = jnp.argmax(dispatch, axis=1)
+
     both_weights = jnp.concatenate([adapter_down_weight[0], adapter_up_weight[0]], axis=0)
     both_full = lax.all_gather(both_weights, "dp", axis=1, tiled=True)
     down_full = both_full[:rank]
     up_full = both_full[rank:]
 
-    rows = jnp.concatenate([tokens, residual], axis=1)
-    placed = jnp.dot(dispatch, rows, preferred_element_type=jnp.float32).astype(jnp.bfloat16)
-    arrived_both = lax.all_to_all(
-        placed.reshape(owner_count, slot_capacity, 2 * width),
-        "owner",
-        split_axis=0,
-        concat_axis=0,
-        tiled=True,
-    ).reshape(slots, 2 * width)
-    arrived = arrived_both[:, :width]
-    arrived_residual = arrived_both[:, width:]
+    def place(row_block):
+        split_rows = row_block.reshape(tok_rows, pieces, piece)
+        picked = jnp.where(valid[:, None, None], split_rows[source], jnp.zeros((), row_block.dtype))
+        return picked.reshape(owner_count, slot_capacity * pieces, piece)
+
+    placed = jnp.concatenate([place(tokens), place(residual)], axis=1)
+    arrived_both = lax.all_to_all(placed, "owner", split_axis=0, concat_axis=0, tiled=True)
+    half = slot_capacity * pieces
+    arrived = arrived_both[:, :half].reshape(slots, width)
+    arrived_residual = arrived_both[:, half:].reshape(slots, width)
 
     hidden_state = lax.dot_general(
         arrived, down_full, (((1,), (1,)), ((), ())), preferred_element_type=jnp.float32

time: 277 us -> 256 us (0.924)
  waiting for transfers between devices: 169 us -> 148 us
  other arithmetic: 10.7 us -> 25.5 us
  starting transfers between devices: 38.8 us -> 24.7 us
  local copies, waits for them, and re-layouts: 21.3 us -> 28.3 us
  matrix products: 21.5 us -> 14.9 us
    all_to_all x1, waiting for transfers between devices: 103 us -> 76.3 us  [body(): lax.all_to_all(placed, 'owner', split_axis=0, concat_axis=0, tiled=True)]
    all_to_all x1, starting transfers between devices: 28.1 us -> 14 us  [body(): lax.all_to_all(slot_loss.reshape(owner_count, slot_capacity), 'owner', sp...]
    reshape x2 -> x1, local copies, waits for them, and re-layouts: 18.1 us -> 4.2 us  [body(): arrived = arrived_both[:, :half].reshape(slots, width)]
    convert_element_type x0 -> x1, other arithmetic: none -> 7.58 us  [body(): arrived_residual.astype(jnp.float32) + adapter_output.astype(jnp.float32)]
    convert_element_type x0 -> x1, local copies, waits for them, and re-layouts: none -> 7.18 us  [body(): arrived_residual.astype(jnp.float32) + adapter_output.astype(jnp.float32)]
    gather x0 -> x2, local copies, waits for them, and re-layouts: none -> 6.94 us  [place(): split_rows[source]]
    dot_general x1 -> x0, matrix products: 6.65 us -> none  [body(): jnp.dot(dispatch, rows, preferred_element_type=jnp.float32)]
    unnamed x16 -> x22, local copies, waits for them, and re-layouts: 0.63 us -> 7.08 us
  transfers between devices with their start and end apart: 4 -> 4, of which waited for: 3 -> 3; matrix products, arithmetic and copies ran while one was open for 5% -> 9% of each run, Pallas kernels for 0% -> 0%
where the time goes in v3:
time: 256 us; the launch traced here: 255 us
  waiting for transfers between devices  148 us (58%)
  local copies, waits for them, and re-layouts  28.3 us (11%)
  other arithmetic  25.5 us (10%)
  starting transfers between devices  24.7 us (10%)
  matrix products  14.9 us (6%)
  between operations  14.2 us (6%)
    all_to_all x1, waiting for transfers between devices, body(): lax.all_to_all(placed, 'owner', split_axis=0, concat_axis=0, tiled=True)  76.3 us
    reduce_scatter x1, waiting for transfers between devices, body(): summed = lax.psum_scatter(both_grads, 'dp', scatter_dimension=1, tiled=True)  65.8 us
    all_to_all x1, starting transfers between devices, body(): lax.all_to_all(slot_loss.reshape(owner_count, slot_capacity), 'owner', sp...  14 us
    all_to_all x1, starting transfers between devices, body(): lax.all_to_all(placed, 'owner', split_axis=0, concat_axis=0, tiled=True)  10.6 us
    convert_element_type x1, other arithmetic, body(): arrived_residual.astype(jnp.float32) + adapter_output.astype(jnp.float32)  7.58 us
    convert_element_type x1, local copies, waits for them, and re-layouts, body(): arrived_residual.astype(jnp.float32) + adapter_output.astype(jnp.float32)  7.18 us
    unnamed x22, local copies, waits for them, and re-layouts  7.08 us
    gather x2, local copies, waits for them, and re-layouts, place(): split_rows[source]  6.94 us
  transfers between devices with their start and end apart: 4, of which 3 were waited for; matrix products, arithmetic and copies ran while one was open for 9% of the time, Pallas kernels for 0%

profile of v3, /device:TPU:6, one launch (start us, length us, event | category | flops | bytes accessed | tf_op | source)
XLA Modules:
  0.0 255.2 jit_solution(1503439096270799338)
XLA Ops:
  7.2 0.7 fusion.32
  8.1 0.8 select_reduce_fusion
  10.7 3.9 %copy.20 = bf16[16,8,16,512]{3,2,1,0:T(8,128)(2,1)} copy(bf16[16,8,16,512]{3,1,2,0:T(8,128)(2,1)} %bitcast.48) | data formatting | bytes 4194304
  14.6 0.8 copy.21
  15.5 4.2 %gather_fusion = bf16[192,16,512]{2,1,0:T(8,128)(2,1)} fusion(bf16[128,16,512]{2,1,0:T(8,128)(2,1)} %bitcast.45, s32[1024]{0:T(1024)S(1)} %pad_clamp_fusion.1), kind=kCustom, calls=%fused_computation | custom fusion | bytes 6292224 | tf_op jit(solution)/shard_map/gather | solution.py:56
  19.7 2.7 %gather_fusion.1 = bf16[192,16,512]{2,1,0:T(8,128)(2,1)} fusion(bf16[128,16,512]{2,1,0:T(8,128)(2,1)S(1)} %bitcast.44, s32[1024]{0:T(1024)S(1)} %pad_clamp_fusion.1), kind=kCustom, calls=%fused_computation.1 | custom fusion | bytes 6292224 | tf_op jit(solution)/shard_map/gather | solution.py:56
  22.4 3.2 %bitcast_select_fusion.1 = (bf16[32,96,512]{2,1,0:T(8,128)(2,1)S(1)}, bf16[32,96,512]{2,1,0:T(8,128)(2,1)S(1)}) fusion(pred[32,96]{1,0:T(8,128)(4,1)S(1)} %copy.18, bf16[32,96,512]{2,1,0:T(8,128)(2,1)} %bitcast.46, bf16[32,96,512]{2,1,0:T(8,128)(2,1)} %bitcast.47), kind=kLoop, calls=%fused_computation.14 | loop fusion | flops 3145728 | bytes 12585984 | tf_op jit(solution)/shard_map/jit(_where)/select_n | solution.py:56
  25.6 3.3 %pad_maximum_fusion = bf16[32,192,512]{2,1,0:T(8,128)(2,1)} fusion(bf16[32,96,512]{2,1,0:T(8,128)(2,1)S(1)} %get-tuple-element.10, bf16[32,96,512]{2,1,0:T(8,128)(2,1)S(1)} %get-tuple-element.9), kind=kLoop, calls=%fused_computation.10 | loop fusion | flops 12582912 | bytes 12582912 | tf_op jit(solution)/shard_map/concatenate | solution.py:59
  28.9 10.6 %all-to-all-start = ((bf16[32,192,512]{2,1,0:T(8,128)(2,1)}), bf16[32,192,512]{2,1,0:T(8,128)(2,1)}, u32[]{:S(2)}, u32[]{:S(2)}) async-start(bf16[32,192,512]{2,1,0:T(8,128)(2,1)} %pad_maximum_fusion), calls=%async_computation | async-start | bytes 12582912 | tf_op jit(solution)/shard_map/all_to_all | solution.py:60
  40.3 76.3 %all-to-all-done = bf16[32,192,512]{2,1,0:T(8,128)(2,1)} async-done(((bf16[32,192,512]{2,1,0:T(8,128)(2,1)}), bf16[32,192,512]{2,1,0:T(8,128)(2,1)}, u32[]{:S(2)}, u32[]{:S(2)}) %all-to-all-start) | async-done | bytes 6291488 | tf_op jit(solution)/shard_map/all_to_all | solution.py:60
  116.7 7.6 %slice_convert_fusion = (f32[32,96,512]{2,1,0:T(8,128)}, bf16[32,96,512]{2,1,0:T(8,128)(2,1)}) fusion(bf16[32,192,512]{2,1,0:T(8,128)(2,1)} %all-to-all-done), kind=kLoop, calls=%fused_computation.12 | loop fusion | flops 1572864 | bytes 15728640 | tf_op jit(solution)/shard_map/convert_element_type | solution.py:71
  124.2 7.2 %reshape.86 = f32[192,8192]{1,0:T(8,128)} reshape(f32[32,96,512]{2,1,0:T(8,128)} %get-tuple-element.5) | data formatting | bytes 12582912 | tf_op jit(solution)/shard_map/convert_element_type | solution.py:71
  131.4 4.2 %reshape.84 = bf16[192,8192]{1,0:T(8,128)(2,1)S(1)} reshape(bf16[32,96,512]{2,1,0:T(8,128)(2,1)} %get-tuple-element.6) | data formatting | bytes 6291456 | tf_op jit(solution)/shard_map/reshape | solution.py:62
  135.7 2.5 convolution_convert_fusion
  138.2 4.5 %fusion.3 = (f32[192]{0:T(256)S(1)}, bf16[192,8192]{1,0:T(8,128)(2,1)S(1)}) fusion(f32[192,8192]{1,0:T(8,128)} %reshape.86, bf16[192,64]{0,1:T(8,128)(2,1)S(1)} %convolution_convert_fusion, bf16[128,8192]{1,0:T(8,128)(2,1)S(1)} %copy-done.1), kind=kOutput, calls=%fused_computation.9 | convolution fusion | flops 213909312 | bytes 10519296 | tf_op jit(solution)/shard_map/dot_general | solution.py:69
  142.6 1.7 copy-done
  144.3 2.0 convolution_multiply_fusion.1
  146.3 5.9 %fusion.14 = f32[64,8192]{1,0:T(8,128)} fusion(bf16[192,8192]{1,0:T(8,128)(2,1)S(1)} %reshape.84, bf16[192,8192]{1,0:T(8,128)(2,1)} %copy-done, bf16[128,8192]{1,0:T(8,128)(2,1)} %all-gather.2.cloned.1.call-done), kind=kOutput, calls=%fused_computation.21 | convolution fusion | flops 402677760 | bytes 9437184 | tf_op jit(solution)/shard_map/dot_general | solution.py:86
  152.2 4.6 %pad_maximum_fusion.1 = f32[128,8192]{1,0:T(8,128)} fusion(f32[64,8192]{1,0:T(8,128)} %convolution_multiply_fusion.1, f32[64,8192]{1,0:T(8,128)} %fusion.14), kind=kLoop, calls=%fused_computation.11 | loop fusion | flops 1048576 | bytes 8388608 | tf_op jit(solution)/shard_map/concatenate | solution.py:90
  158.2 14.0 %all-to-all-start.1 = ((f32[32,1,6]{2,1,0:T(1,128)}), f32[32,1,6]{2,1,0:T(1,128)S(1)}, u32[]{:S(2)}, u32[]{:S(2)}) async-start(f32[32,1,6]{2,1,0:T(1,128)} %bitcast.14), calls=%async_computation.2 | async-start | bytes 32768 | tf_op jit(solution)/shard_map/all_to_all | solution.py:97
  172.2 5.4 %all-to-all-done.1 = f32[32,1,6]{2,1,0:T(1,128)S(1)} async-done(((f32[32,1,6]{2,1,0:T(1,128)}), f32[32,1,6]{2,1,0:T(1,128)S(1)}, u32[]{:S(2)}, u32[]{:S(2)}) %all-to-all-start.1) | async-done | bytes 800 | tf_op jit(solution)/shard_map/all_to_all | solution.py:97
  178.9 1.3 gather_fusion.2
  180.7 65.8 %reduce-scatter.2.cloned.1.call-done = f32[128,512]{1,0:T(8,128)} async-done(((f32[128,8192]{1,0:T(8,128)}), f32[128,512]{1,0:T(8,128)}) %reduce-scatter.2.cloned.1.call-update) | async-done | bytes 262160 | tf_op jit(solution)/shard_map/reduce_scatter | solution.py:91
  246.5 1.8 fusion.29
  (44 shorter events, 5.9 us)
Async XLA Ops:
  10.7 4.0 %copy-start.2 = (bf16[128,8192]{1,0:T(8,128)(2,1)S(1)}, bf16[128,8192]{1,0:T(8,128)(2,1)}, u32[]{:S(2)}) copy-start(bf16[128,8192]{1,0:T(8,128)(2,1)} %param.10) | copy-start | bytes 6291460
  28.9 10.7 %copy-start.7 = (bf16[1,64,512]{2,1,0:T(8,128)(2,1)S(1)}, bf16[1,64,512]{2,1,0:T(8,128)(2,1)}, u32[]{:S(2)}) copy-start(bf16[1,64,512]{2,1,0:T(8,128)(2,1)} %param.13) | copy-start | bytes 196612
  28.9 10.7 %copy-start.8 = (bf16[1,64,512]{2,1,0:T(8,128)(2,1)S(1)}, bf16[1,64,512]{2,1,0:T(8,128)(2,1)}, u32[]{:S(2)}) copy-start(bf16[1,64,512]{2,1,0:T(8,128)(2,1)} %param.12) | copy-start | bytes 196612
  28.9 87.7 %all-to-all-start = ((bf16[32,192,512]{2,1,0:T(8,128)(2,1)}), bf16[32,192,512]{2,1,0:T(8,128)(2,1)}, u32[]{:S(2)}, u32[]{:S(2)}) async-start(bf16[32,192,512]{2,1,0:T(8,128)(2,1)} %pad_maximum_fusion), calls=%async_computation | async-start | bytes 12582912 | tf_op jit(solution)/shard_map/all_to_all | solution.py:60
  39.5 96.1 %all-gather.2.cloned.1.call-start = ((), (), s32[]{:S(2)}) async-start(), calls=%async_computation.3 | async-start | bytes 2228224 | tf_op jit(solution)/shard_map/all_gather | solution.py:50
  40.3 206.2 %reduce-scatter.2.cloned.1.call-start = ((), (), s32[]{:S(2)}) async-start(), calls=%async_computation.4 | async-start | bytes 4456448 | tf_op jit(solution)/shard_map/reduce_scatter | solution.py:91
  135.6 2.5 copy-start.1
  142.6 1.7 copy-start
  156.8 0.7 copy-start.9
  156.8 89.7 %copy-start.3 = (bf16[1,64,512]{2,1,0:T(8,128)(2,1)S(1)}, bf16[1,64,512]{2,1,0:T(8,128)(2,1)}, u32[]{:S(2)}) copy-start(bf16[1,64,512]{2,1,0:T(8,128)(2,1)} %param.17) | copy-start | bytes 196612
  156.8 89.7 %copy-start.4 = (bf16[1,64,512]{2,1,0:T(8,128)(2,1)S(1)}, bf16[1,64,512]{2,1,0:T(8,128)(2,1)}, u32[]{:S(2)}) copy-start(bf16[1,64,512]{2,1,0:T(8,128)(2,1)} %param.16) | copy-start | bytes 196612
  156.8 89.7 %copy-start.5 = (bf16[1,64,512]{2,1,0:T(8,128)(2,1)S(1)}, bf16[1,64,512]{2,1,0:T(8,128)(2,1)}, u32[]{:S(2)}) copy-start(bf16[1,64,512]{2,1,0:T(8,128)(2,1)} %param.15) | copy-start | bytes 196612
  156.8 89.7 %copy-start.6 = (bf16[1,64,512]{2,1,0:T(8,128)(2,1)S(1)}, bf16[1,64,512]{2,1,0:T(8,128)(2,1)}, u32[]{:S(2)}) copy-start(bf16[1,64,512]{2,1,0:T(8,128)(2,1)} %param.14) | copy-start | bytes 196612
  158.2 19.4 %all-to-all-start.1 = ((f32[32,1,6]{2,1,0:T(1,128)}), f32[32,1,6]{2,1,0:T(1,128)S(1)}, u32[]{:S(2)}, u32[]{:S(2)}) async-start(f32[32,1,6]{2,1,0:T(1,128)} %bitcast.14), calls=%async_computation.2 | async-start | bytes 32768 | tf_op jit(solution)/shard_map/all_to_all | solution.py:97
Sparse Core Ops, SparseCore 0:
  43.0 74.0 all-gather.1
  156.9 89.5 reduce-scatter.1

commit v4 on v3

--- a/solution.py
+++ b/solution.py
@@ -56,11 +56,11 @@
         picked = jnp.where(valid[:, None, None], split_rows[source], jnp.zeros((), row_block.dtype))
         return picked.reshape(owner_count, slot_capacity * pieces, piece)
 
-    placed = jnp.concatenate([place(tokens), place(residual)], axis=1)
-    arrived_both = lax.all_to_all(placed, "owner", split_axis=0, concat_axis=0, tiled=True)
-    half = slot_capacity * pieces
-    arrived = arrived_both[:, :half].reshape(slots, width)
-    arrived_residual = arrived_both[:, half:].reshape(slots, width)
+    def send(row_block):
+        return lax.all_to_all(place(row_block), "owner", split_axis=0, concat_axis=0, tiled=True)
+
+    arrived = send(tokens).reshape(slots, width)
+    arrived_residual = lax.optimization_barrier(send(residual).reshape(slots, width))
 
     hidden_state = lax.dot_general(
         arrived, down_full, (((1,), (1,)), ((), ())), preferred_element_type=jnp.float32

time: 256 us -> 235 us (0.918)
  other arithmetic: 25.5 us -> 16.5 us
  waiting for transfers between devices: 148 us -> 143 us
  local copies, waits for them, and re-layouts: 28.3 us -> 24.4 us
    all_to_all x1, starting transfers between devices: 14 us -> 5.88 us  [body(): lax.all_to_all(slot_loss.reshape(owner_count, slot_capacity), 'owner', sp...]
    convert_element_type x1 -> x0, other arithmetic: 7.58 us -> none  [body(): arrived_residual.astype(jnp.float32) + adapter_output.astype(jnp.float32)]
    convert_element_type x1 -> x0, local copies, waits for them, and re-layouts: 7.18 us -> none  [body(): arrived_residual.astype(jnp.float32) + adapter_output.astype(jnp.float32)]
    all_to_all x1 -> x2, starting transfers between devices: 10.6 us -> 16.6 us  [send(): lax.all_to_all(place(row_block), 'owner', split_axis=0, concat_axis=0, ti...]
    all_to_all x1 -> x2, waiting for transfers between devices: 76.3 us -> 72.1 us  [send(): lax.all_to_all(place(row_block), 'owner', split_axis=0, concat_axis=0, ti...]
    reshape x1 -> x2, local copies, waits for them, and re-layouts: 4.2 us -> 7.7 us  [the longest x1 4.2 us: body(): arrived = send(tokens).reshape(slots, width)]
    concatenate x1 -> x0, other arithmetic: 3.31 us -> none  [body(): placed = jnp.concatenate([place(tokens), place(residual)], axis=1)]
  transfers between devices with their start and end apart: 4 -> 5, of which waited for: 3 -> 4; matrix products, arithmetic and copies ran while one was open for 9% -> 5% of each run, Pallas kernels for 0% -> 0%
where the time goes in v4:
time: 235 us
  waiting for transfers between devices  143 us (61%)
  local copies, waits for them, and re-layouts  24.4 us (10%)
  starting transfers between devices  22.5 us (10%)
  other arithmetic  16.5 us (7%)
  between operations  14.2 us (6%)
  matrix products  13.6 us (6%)
    all_to_all x2, waiting for transfers between devices, send(): lax.all_to_all(place(row_block), 'owner', split_axis=0, concat_axis=0, ti...  72.1 us
    reduce_scatter x1, waiting for transfers between devices, body(): summed = lax.psum_scatter(both_grads, 'dp', scatter_dimension=1, tiled=True)  65.8 us
    all_to_all x2, starting transfers between devices, send(): lax.all_to_all(place(row_block), 'owner', split_axis=0, concat_axis=0, ti...  16.6 us
    unnamed x22, local copies, waits for them, and re-layouts  6.91 us
    gather x2, local copies, waits for them, and re-layouts, place(): split_rows[source]  6.9 us
    dot_general x1, matrix products, body(): lax.dot_general(hidden_gradient, arrived, (((0,), (0,)), ((), ())), prefe...  5.88 us
    all_to_all x1, starting transfers between devices, body(): lax.all_to_all(slot_loss.reshape(owner_count, slot_capacity), 'owner', sp...  5.88 us
    all_to_all x1, waiting for transfers between devices, body(): lax.all_to_all(slot_loss.reshape(owner_count, slot_capacity), 'owner', sp...  5.41 us
  transfers between devices with their start and end apart: 5, of which 4 were waited for; matrix products, arithmetic and copies ran while one was open for 5% of the time, Pallas kernels for 0%

profile of v4, /device:TPU:6, one launch (start us, length us, event | category | flops | bytes accessed | tf_op | source)
XLA Modules:
  0.0 234.6 jit_solution(3856146406854847340)
XLA Ops:
  7.2 0.7 fusion.32
  8.1 1.0 select_reduce_fusion
  10.5 3.8 %copy.21 = bf16[16,8,16,512]{3,2,1,0:T(8,128)(2,1)} copy(bf16[16,8,16,512]{3,1,2,0:T(8,128)(2,1)} %bitcast.48) | data formatting | bytes 4194304
  14.3 0.8 copy.20
  15.1 4.3 %gather_fusion.1 = bf16[192,16,512]{2,1,0:T(8,128)(2,1)} fusion(bf16[128,16,512]{2,1,0:T(8,128)(2,1)} %bitcast.45, s32[1024]{0:T(1024)S(1)} %pad_clamp_fusion.1), kind=kCustom, calls=%fused_computation.1 | custom fusion | bytes 6292224 | tf_op jit(solution)/shard_map/gather | solution.py:56
  19.4 2.6 %gather_fusion = bf16[192,16,512]{2,1,0:T(8,128)(2,1)} fusion(bf16[128,16,512]{2,1,0:T(8,128)(2,1)S(1)} %bitcast.44, s32[1024]{0:T(1024)S(1)} %pad_clamp_fusion.1), kind=kCustom, calls=%fused_computation | custom fusion | bytes 6292224 | tf_op jit(solution)/shard_map/gather | solution.py:56
  22.4 4.9 %bitcast_select_fusion.1 = (bf16[32,96,512]{2,1,0:T(8,128)(2,1)}, bf16[32,96,512]{2,1,0:T(8,128)(2,1)}) fusion(pred[32,96]{1,0:T(8,128)(4,1)S(1)} %copy.18, bf16[32,96,512]{2,1,0:T(8,128)(2,1)} %bitcast.47, bf16[32,96,512]{2,1,0:T(8,128)(2,1)} %bitcast.46), kind=kLoop, calls=%fused_computation.12 | loop fusion | flops 3145728 | bytes 12585984 | tf_op jit(solution)/shard_map/jit(_where)/select_n | solution.py:56
  27.3 9.8 %all-to-all-start = ((bf16[32,96,512]{2,1,0:T(8,128)(2,1)}), bf16[32,96,512]{2,1,0:T(8,128)(2,1)S(1)}, u32[]{:S(2)}, u32[]{:S(2)}) async-start(bf16[32,96,512]{2,1,0:T(8,128)(2,1)} %get-tuple-element.7), calls=%async_computation | async-start | bytes 6291456 | tf_op jit(solution)/shard_map/all_to_all | solution.py:60
  37.9 37.4 %all-to-all-done = bf16[32,96,512]{2,1,0:T(8,128)(2,1)S(1)} async-done(((bf16[32,96,512]{2,1,0:T(8,128)(2,1)}), bf16[32,96,512]{2,1,0:T(8,128)(2,1)S(1)}, u32[]{:S(2)}, u32[]{:S(2)}) %all-to-all-start) | async-done | bytes 3145760 | tf_op jit(solution)/shard_map/all_to_all | solution.py:60
  75.3 6.7 %all-to-all-start.1 = ((bf16[32,96,512]{2,1,0:T(8,128)(2,1)}), bf16[32,96,512]{2,1,0:T(8,128)(2,1)}, u32[]{:S(2)}, u32[]{:S(2)}) async-start(bf16[32,96,512]{2,1,0:T(8,128)(2,1)} %get-tuple-element.8), calls=%async_computation.1 | async-start | bytes 6291456 | tf_op jit(solution)/shard_map/all_to_all | solution.py:60
  82.1 3.5 %reshape.83 = bf16[192,8192]{1,0:T(8,128)(2,1)} reshape(bf16[32,96,512]{2,1,0:T(8,128)(2,1)S(1)} %all-to-all-done) | data formatting | bytes 6291456 | tf_op jit(solution)/shard_map/reshape | solution.py:63
  85.6 34.7 %all-to-all-done.1 = bf16[32,96,512]{2,1,0:T(8,128)(2,1)} async-done(((bf16[32,96,512]{2,1,0:T(8,128)(2,1)}), bf16[32,96,512]{2,1,0:T(8,128)(2,1)}, u32[]{:S(2)}, u32[]{:S(2)}) %all-to-all-start.1) | async-done | bytes 3145760 | tf_op jit(solution)/shard_map/all_to_all | solution.py:60
  120.3 4.2 %reshape.85 = bf16[192,8192]{1,0:T(8,128)(2,1)S(1)} reshape(bf16[32,96,512]{2,1,0:T(8,128)(2,1)} %all-to-all-done.1) | data formatting | bytes 6291456 | tf_op jit(solution)/shard_map/reshape | solution.py:62
  124.6 2.5 %convolution_convert_fusion = bf16[192,64]{0,1:T(8,128)(2,1)S(1)} fusion(bf16[192,8192]{1,0:T(8,128)(2,1)S(1)} %reshape.85, bf16[128,8192]{1,0:T(8,128)(2,1)} %all-gather.2.cloned.1.call-done), kind=kOutput, calls=%fused_computation.18 | convolution fusion | flops 201338880 | bytes 4218880 | tf_op jit(solution)/shard_map/dot_general | solution.py:65
  127.1 3.1 %fusion.3 = (f32[192]{0:T(256)S(1)}, bf16[192,8192]{1,0:T(8,128)(2,1)S(1)}) fusion(bf16[192,64]{0,1:T(8,128)(2,1)S(1)} %convolution_convert_fusion, bf16[128,8192]{1,0:T(8,128)(2,1)} %all-gather.2.cloned.1.call-done, bf16[192,8192]{1,0:T(8,128)(2,1)S(1)} %copy-done.1), kind=kOutput, calls=%fused_computation.9 | convolution fusion | flops 215482176 | bytes 7365376 | tf_op jit(solution)/shard_map/dot_general | solution.py:69
  130.2 1.7 copy-done
  131.9 2.0 convolution_multiply_fusion.1
  133.9 5.9 %fusion.14 = f32[64,8192]{1,0:T(8,128)} fusion(bf16[192,8192]{1,0:T(8,128)(2,1)S(1)} %reshape.85, bf16[192,8192]{1,0:T(8,128)(2,1)} %copy-done, bf16[128,8192]{1,0:T(8,128)(2,1)} %all-gather.2.cloned.1.call-done), kind=kOutput, calls=%fused_computation.19 | convolution fusion | flops 402677760 | bytes 9437184 | tf_op jit(solution)/shard_map/dot_general | solution.py:86
  139.8 4.6 %pad_maximum_fusion = f32[128,8192]{1,0:T(8,128)} fusion(f32[64,8192]{1,0:T(8,128)} %convolution_multiply_fusion.1, f32[64,8192]{1,0:T(8,128)} %fusion.14), kind=kLoop, calls=%fused_computation.10 | loop fusion | flops 1048576 | bytes 8388608 | tf_op jit(solution)/shard_map/concatenate | solution.py:90
  145.7 5.9 %all-to-all-start.2 = ((f32[32,1,6]{2,1,0:T(1,128)}), f32[32,1,6]{2,1,0:T(1,128)S(1)}, u32[]{:S(2)}, u32[]{:S(2)}) async-start(f32[32,1,6]{2,1,0:T(1,128)} %bitcast.14), calls=%async_computation.3 | async-start | bytes 32768 | tf_op jit(solution)/shard_map/all_to_all | solution.py:97
  151.6 5.4 %all-to-all-done.2 = f32[32,1,6]{2,1,0:T(1,128)S(1)} async-done(((f32[32,1,6]{2,1,0:T(1,128)}), f32[32,1,6]{2,1,0:T(1,128)S(1)}, u32[]{:S(2)}, u32[]{:S(2)}) %all-to-all-start.2) | async-done | bytes 800 | tf_op jit(solution)/shard_map/all_to_all | solution.py:97
  158.4 1.3 gather_fusion.2
  160.1 65.8 %reduce-scatter.2.cloned.1.call-done = f32[128,512]{1,0:T(8,128)} async-done(((f32[128,8192]{1,0:T(8,128)}), f32[128,512]{1,0:T(8,128)}) %reduce-scatter.2.cloned.1.call-update) | async-done | bytes 262160 | tf_op jit(solution)/shard_map/reduce_scatter | solution.py:91
  225.9 1.8 fusion.29
  (44 shorter events, 5.9 us)
Async XLA Ops:
  8.1 6.2 %copy-start.2 = (bf16[128,8192]{1,0:T(8,128)(2,1)S(1)}, bf16[128,8192]{1,0:T(8,128)(2,1)}, u32[]{:S(2)}) copy-start(bf16[128,8192]{1,0:T(8,128)(2,1)} %param.10) | copy-start | bytes 6291460
  27.3 9.9 %copy-start.7 = (bf16[1,64,512]{2,1,0:T(8,128)(2,1)S(1)}, bf16[1,64,512]{2,1,0:T(8,128)(2,1)}, u32[]{:S(2)}) copy-start(bf16[1,64,512]{2,1,0:T(8,128)(2,1)} %param.13) | copy-start | bytes 196612
  27.3 9.9 %copy-start.8 = (bf16[1,64,512]{2,1,0:T(8,128)(2,1)S(1)}, bf16[1,64,512]{2,1,0:T(8,128)(2,1)}, u32[]{:S(2)}) copy-start(bf16[1,64,512]{2,1,0:T(8,128)(2,1)} %param.12) | copy-start | bytes 196612
  27.3 48.0 %all-to-all-start = ((bf16[32,96,512]{2,1,0:T(8,128)(2,1)}), bf16[32,96,512]{2,1,0:T(8,128)(2,1)S(1)}, u32[]{:S(2)}, u32[]{:S(2)}) async-start(bf16[32,96,512]{2,1,0:T(8,128)(2,1)} %get-tuple-element.7), calls=%async_computation | async-start | bytes 6291456 | tf_op jit(solution)/shard_map/all_to_all | solution.py:60
  37.1 87.4 %all-gather.2.cloned.1.call-start = ((), (), s32[]{:S(2)}) async-start(), calls=%async_computation.4 | async-start | bytes 2228224 | tf_op jit(solution)/shard_map/all_gather | solution.py:50
  75.3 45.0 %all-to-all-start.1 = ((bf16[32,96,512]{2,1,0:T(8,128)(2,1)}), bf16[32,96,512]{2,1,0:T(8,128)(2,1)}, u32[]{:S(2)}, u32[]{:S(2)}) async-start(bf16[32,96,512]{2,1,0:T(8,128)(2,1)} %get-tuple-element.8), calls=%async_computation.1 | async-start | bytes 6291456 | tf_op jit(solution)/shard_map/all_to_all | solution.py:60
  82.1 143.9 %reduce-scatter.2.cloned.1.call-start = ((), (), s32[]{:S(2)}) async-start(), calls=%async_computation.5 | async-start | bytes 4456448 | tf_op jit(solution)/shard_map/reduce_scatter | solution.py:91
  124.5 2.5 %copy-start.1 = (bf16[192,8192]{1,0:T(8,128)(2,1)S(1)}, bf16[192,8192]{1,0:T(8,128)(2,1)}, u32[]{:S(2)}) copy-start(bf16[192,8192]{1,0:T(8,128)(2,1)} %reshape.83) | copy-start | bytes 9437188
  130.2 1.7 copy-start
  144.4 0.7 copy-start.9
  144.4 81.6 %copy-start.3 = (bf16[1,64,512]{2,1,0:T(8,128)(2,1)S(1)}, bf16[1,64,512]{2,1,0:T(8,128)(2,1)}, u32[]{:S(2)}) copy-start(bf16[1,64,512]{2,1,0:T(8,128)(2,1)} %param.17) | copy-start | bytes 196612
  144.4 81.6 %copy-start.4 = (bf16[1,64,512]{2,1,0:T(8,128)(2,1)S(1)}, bf16[1,64,512]{2,1,0:T(8,128)(2,1)}, u32[]{:S(2)}) copy-start(bf16[1,64,512]{2,1,0:T(8,128)(2,1)} %param.16) | copy-start | bytes 196612
  144.4 81.6 %copy-start.5 = (bf16[1,64,512]{2,1,0:T(8,128)(2,1)S(1)}, bf16[1,64,512]{2,1,0:T(8,128)(2,1)}, u32[]{:S(2)}) copy-start(bf16[1,64,512]{2,1,0:T(8,128)(2,1)} %param.15) | copy-start | bytes 196612
  144.4 81.6 %copy-start.6 = (bf16[1,64,512]{2,1,0:T(8,128)(2,1)S(1)}, bf16[1,64,512]{2,1,0:T(8,128)(2,1)}, u32[]{:S(2)}) copy-start(bf16[1,64,512]{2,1,0:T(8,128)(2,1)} %param.14) | copy-start | bytes 196612
  145.7 11.3 %all-to-all-start.2 = ((f32[32,1,6]{2,1,0:T(1,128)}), f32[32,1,6]{2,1,0:T(1,128)S(1)}, u32[]{:S(2)}, u32[]{:S(2)}) async-start(f32[32,1,6]{2,1,0:T(1,128)} %bitcast.14), calls=%async_computation.3 | async-start | bytes 32768 | tf_op jit(solution)/shard_map/all_to_all | solution.py:97
Sparse Core Ops, SparseCore 0:
  40.6 74.9 all-gather.1
  144.5 81.3 reduce-scatter.1

commit v5 on v4

--- a/solution.py
+++ b/solution.py
@@ -59,8 +59,13 @@
     def send(row_block):
         return lax.all_to_all(place(row_block), "owner", split_axis=0, concat_axis=0, tiled=True)
 
-    arrived = send(tokens).reshape(slots, width)
-    arrived_residual = lax.optimization_barrier(send(residual).reshape(slots, width))
+    arrived_tokens = send(tokens)
+    placed_residual, arrived_tokens = lax.optimization_barrier((place(residual), arrived_tokens))
+    arrived = arrived_tokens.reshape(slots, width)
+    arrived_residual = lax.all_to_all(
+        placed_residual, "owner", split_axis=0, concat_axis=0, tiled=True
+    )
+    arrived_residual = lax.optimization_barrier(arrived_residual.reshape(slots, width))
 
     hidden_state = lax.dot_general(
         arrived, down_full, (((1,), (1,)), ((), ())), preferred_element_type=jnp.float32

time: 235 us -> 237 us (level)
  local copies, waits for them, and re-layouts: 24.4 us -> 28.5 us
  waiting for transfers between devices: 143 us -> 140 us
    all_to_all x2 -> x1, waiting for transfers between devices: 72.1 us -> 37.4 us  [send(): lax.all_to_all(place(row_block), 'owner', split_axis=0, concat_axis=0, ti...]
    all_gather x1, waiting for transfers between devices: 0.02 us -> 27.5 us  [body(): both_full = lax.all_gather(both_weights, 'dp', axis=1, tiled=True)]
    all_to_all x0 -> x1, starting transfers between devices: none -> 6.75 us  [body(): lax.all_to_all(placed_residual, 'owner', split_axis=0, concat_axis=0, til...]
    all_to_all x2 -> x1, starting transfers between devices: 16.6 us -> 9.83 us  [send(): lax.all_to_all(place(row_block), 'owner', split_axis=0, concat_axis=0, ti...]
    all_to_all x0 -> x1, waiting for transfers between devices: none -> 4.1 us  [body(): lax.all_to_all(placed_residual, 'owner', split_axis=0, concat_axis=0, til...]
    reshape x2, local copies, waits for them, and re-layouts: 7.7 us -> 10.1 us  [the longest x1 5.89 us: body(): arrived_residual.reshape(slots, width)]
  transfers between devices with their start and end apart: 5 -> 5, of which waited for: 4 -> 5; matrix products, arithmetic and copies ran while one was open for 5% -> 5% of each run, Pallas kernels for 0% -> 0%
where the time goes in v5:
time: 237 us; the launch traced here: 236 us
  waiting for transfers between devices  140 us (59%)
  local copies, waits for them, and re-layouts  28.5 us (12%)
  starting transfers between devices  22.6 us (10%)
  other arithmetic  16.5 us (7%)
  matrix products  14.3 us (6%)
  between operations  14.2 us (6%)
    reduce_scatter x1, waiting for transfers between devices, body(): summed = lax.psum_scatter(both_grads, 'dp', scatter_dimension=1, tiled=True)  65.7 us
    all_to_all x1, waiting for transfers between devices, send(): lax.all_to_all(place(row_block), 'owner', split_axis=0, concat_axis=0, ti...  37.4 us
    all_gather x1, waiting for transfers between devices, body(): both_full = lax.all_gather(both_weights, 'dp', axis=1, tiled=True)  27.5 us
    all_to_all x1, starting transfers between devices, send(): lax.all_to_all(place(row_block), 'owner', split_axis=0, concat_axis=0, ti...  9.83 us
    unnamed x22, local copies, waits for them, and re-layouts  8.61 us
    gather x2, local copies, waits for them, and re-layouts, place(): split_rows[source]  6.9 us
    all_to_all x1, starting transfers between devices, body(): lax.all_to_all(placed_residual, 'owner', split_axis=0, concat_axis=0, til...  6.75 us
    all_to_all x1, starting transfers between devices, body(): lax.all_to_all(slot_loss.reshape(owner_count, slot_capacity), 'owner', sp...  5.9 us
  transfers between devices with their start and end apart: 5, of which 5 were waited for; matrix products, arithmetic and copies ran while one was open for 5% of the time, Pallas kernels for 0%

profile of v5, /device:TPU:6, one launch (start us, length us, event | category | flops | bytes accessed | tf_op | source)
XLA Modules:
  0.0 236.3 jit_solution(3586301800810176762)
XLA Ops:
  8.1 1.0 select_reduce_fusion
  10.5 3.8 %copy.20 = bf16[16,8,16,512]{3,2,1,0:T(8,128)(2,1)} copy(bf16[16,8,16,512]{3,1,2,0:T(8,128)(2,1)} %bitcast.48) | data formatting | bytes 4194304
  15.1 4.3 %gather_fusion = bf16[192,16,512]{2,1,0:T(8,128)(2,1)} fusion(bf16[128,16,512]{2,1,0:T(8,128)(2,1)} %bitcast.45, s32[1024]{0:T(1024)S(1)} %pad_clamp_fusion.1), kind=kCustom, calls=%fused_computation | custom fusion | bytes 6292224 | tf_op jit(solution)/shard_map/gather | solution.py:56
  19.4 2.6 %gather_fusion.1 = bf16[192,16,512]{2,1,0:T(8,128)(2,1)} fusion(bf16[128,16,512]{2,1,0:T(8,128)(2,1)S(1)} %bitcast.44, s32[1024]{0:T(1024)S(1)} %pad_clamp_fusion.1), kind=kCustom, calls=%fused_computation.1 | custom fusion | bytes 6292224 | tf_op jit(solution)/shard_map/gather | solution.py:56
  22.4 4.9 %bitcast_select_fusion = (bf16[32,96,512]{2,1,0:T(8,128)(2,1)}, bf16[32,96,512]{2,1,0:T(8,128)(2,1)}) fusion(pred[32,96]{1,0:T(8,128)(4,1)S(1)} %copy.18, bf16[32,96,512]{2,1,0:T(8,128)(2,1)} %bitcast.47, bf16[32,96,512]{2,1,0:T(8,128)(2,1)} %bitcast.46), kind=kLoop, calls=%fused_computation.11 | loop fusion | flops 3145728 | bytes 12585984 | tf_op jit(solution)/shard_map/jit(_where)/select_n | solution.py:56
  27.3 9.8 %all-to-all-start = ((bf16[32,96,512]{2,1,0:T(8,128)(2,1)}), bf16[32,96,512]{2,1,0:T(8,128)(2,1)S(1)}, u32[]{:S(2)}, u32[]{:S(2)}) async-start(bf16[32,96,512]{2,1,0:T(8,128)(2,1)} %get-tuple-element.11), calls=%async_computation | async-start | bytes 6291456 | tf_op jit(solution)/shard_map/all_to_all | solution.py:60
  37.9 37.4 %all-to-all-done = bf16[32,96,512]{2,1,0:T(8,128)(2,1)S(1)} async-done(((bf16[32,96,512]{2,1,0:T(8,128)(2,1)}), bf16[32,96,512]{2,1,0:T(8,128)(2,1)S(1)}, u32[]{:S(2)}, u32[]{:S(2)}) %all-to-all-start) | async-done | bytes 3145760 | tf_op jit(solution)/shard_map/all_to_all | solution.py:60
  75.3 1.7 copy-done
  77.0 6.7 %all-to-all-start.1 = ((bf16[32,96,512]{2,1,0:T(8,128)(2,1)}), bf16[32,96,512]{2,1,0:T(8,128)(2,1)}, u32[]{:S(2)}, u32[]{:S(2)}) async-start(bf16[32,96,512]{2,1,0:T(8,128)(2,1)} %get-tuple-element.7), calls=%async_computation.1 | async-start | bytes 6291456 | tf_op jit(solution)/shard_map/all_to_all | solution.py:65
  83.8 4.2 %reshape.85 = bf16[192,8192]{1,0:T(8,128)(2,1)S(1)} reshape(bf16[32,96,512]{2,1,0:T(8,128)(2,1)} %copy-done) | data formatting | bytes 6291456 | tf_op jit(solution)/shard_map/reshape | solution.py:64
  88.0 27.5 %all-gather.2.cloned.1.call-done = bf16[128,8192]{1,0:T(8,128)(2,1)} async-done(((bf16[128,512]{1,0:T(8,128)(2,1)}), bf16[128,8192]{1,0:T(8,128)(2,1)}) %all-gather.2.cloned.1.call-update) | async-done | bytes 2097168 | tf_op jit(solution)/shard_map/all_gather | solution.py:50
  115.6 2.3 convolution_convert_fusion
  117.9 4.1 %all-to-all-done.1 = bf16[32,96,512]{2,1,0:T(8,128)(2,1)} async-done(((bf16[32,96,512]{2,1,0:T(8,128)(2,1)}), bf16[32,96,512]{2,1,0:T(8,128)(2,1)}, u32[]{:S(2)}, u32[]{:S(2)}) %all-to-all-start.1) | async-done | bytes 3145760 | tf_op jit(solution)/shard_map/all_to_all | solution.py:65
  122.0 5.9 %reshape.84 = bf16[192,8192]{1,0:T(8,128)(2,1)} reshape(bf16[32,96,512]{2,1,0:T(8,128)(2,1)} %all-to-all-done.1) | data formatting | bytes 6291456 | tf_op jit(solution)/shard_map/reshape | solution.py:68
  127.9 4.1 %fusion.3 = (f32[192]{0:T(256)S(1)}, bf16[192,8192]{1,0:T(8,128)(2,1)S(1)}) fusion(bf16[192,64]{0,1:T(8,128)(2,1)S(1)} %convolution_convert_fusion, bf16[128,8192]{1,0:T(8,128)(2,1)} %all-gather.2.cloned.1.call-done, bf16[192,8192]{1,0:T(8,128)(2,1)} %reshape.84), kind=kOutput, calls=%fused_computation.9 | convolution fusion | flops 215482176 | bytes 7365376 | tf_op jit(solution)/shard_map/dot_general | solution.py:74
  132.0 1.7 copy-done.1
  133.7 2.0 convolution_multiply_fusion.1
  135.7 5.9 %fusion.14 = f32[64,8192]{1,0:T(8,128)} fusion(bf16[192,8192]{1,0:T(8,128)(2,1)S(1)} %reshape.85, bf16[192,8192]{1,0:T(8,128)(2,1)} %copy-done.1, bf16[128,8192]{1,0:T(8,128)(2,1)} %all-gather.2.cloned.1.call-done), kind=kOutput, calls=%fused_computation.19 | convolution fusion | flops 402677760 | bytes 9437184 | tf_op jit(solution)/shard_map/dot_general | solution.py:91
  141.6 4.6 %pad_maximum_fusion = f32[128,8192]{1,0:T(8,128)} fusion(f32[64,8192]{1,0:T(8,128)} %convolution_multiply_fusion.1, f32[64,8192]{1,0:T(8,128)} %fusion.14), kind=kLoop, calls=%fused_computation.10 | loop fusion | flops 1048576 | bytes 8388608 | tf_op jit(solution)/shard_map/concatenate | solution.py:95
  147.5 5.9 %all-to-all-start.2 = ((f32[32,1,6]{2,1,0:T(1,128)}), f32[32,1,6]{2,1,0:T(1,128)S(1)}, u32[]{:S(2)}, u32[]{:S(2)}) async-start(f32[32,1,6]{2,1,0:T(1,128)} %bitcast.14), calls=%async_computation.3 | async-start | bytes 32768 | tf_op jit(solution)/shard_map/all_to_all | solution.py:102
  153.4 5.4 %all-to-all-done.2 = f32[32,1,6]{2,1,0:T(1,128)S(1)} async-done(((f32[32,1,6]{2,1,0:T(1,128)}), f32[32,1,6]{2,1,0:T(1,128)S(1)}, u32[]{:S(2)}, u32[]{:S(2)}) %all-to-all-start.2) | async-done | bytes 800 | tf_op jit(solution)/shard_map/all_to_all | solution.py:102
  160.2 1.3 gather_fusion.2
  161.9 65.7 %reduce-scatter.2.cloned.1.call-done = f32[128,512]{1,0:T(8,128)} async-done(((f32[128,8192]{1,0:T(8,128)}), f32[128,512]{1,0:T(8,128)}) %reduce-scatter.2.cloned.1.call-update) | async-done | bytes 262160 | tf_op jit(solution)/shard_map/reduce_scatter | solution.py:96
  227.6 1.8 fusion.29
  (44 shorter events, 7.4 us)
Async XLA Ops:
  8.1 6.2 %copy-start.2 = (bf16[128,8192]{1,0:T(8,128)(2,1)S(1)}, bf16[128,8192]{1,0:T(8,128)(2,1)}, u32[]{:S(2)}) copy-start(bf16[128,8192]{1,0:T(8,128)(2,1)} %param.9) | copy-start | bytes 6291460
  27.3 9.9 %copy-start.7 = (bf16[1,64,512]{2,1,0:T(8,128)(2,1)S(1)}, bf16[1,64,512]{2,1,0:T(8,128)(2,1)}, u32[]{:S(2)}) copy-start(bf16[1,64,512]{2,1,0:T(8,128)(2,1)} %param.13) | copy-start | bytes 196612
  27.3 9.9 %copy-start.8 = (bf16[1,64,512]{2,1,0:T(8,128)(2,1)S(1)}, bf16[1,64,512]{2,1,0:T(8,128)(2,1)}, u32[]{:S(2)}) copy-start(bf16[1,64,512]{2,1,0:T(8,128)(2,1)} %param.12) | copy-start | bytes 196612
  27.3 48.0 %all-to-all-start = ((bf16[32,96,512]{2,1,0:T(8,128)(2,1)}), bf16[32,96,512]{2,1,0:T(8,128)(2,1)S(1)}, u32[]{:S(2)}, u32[]{:S(2)}) async-start(bf16[32,96,512]{2,1,0:T(8,128)(2,1)} %get-tuple-element.11), calls=%async_computation | async-start | bytes 6291456 | tf_op jit(solution)/shard_map/all_to_all | solution.py:60
  37.1 78.5 %all-gather.2.cloned.1.call-start = ((), (), s32[]{:S(2)}) async-start(), calls=%async_computation.4 | async-start | bytes 2228224 | tf_op jit(solution)/shard_map/all_gather | solution.py:50
  75.3 1.7 copy-start
  77.0 45.0 %all-to-all-start.1 = ((bf16[32,96,512]{2,1,0:T(8,128)(2,1)}), bf16[32,96,512]{2,1,0:T(8,128)(2,1)}, u32[]{:S(2)}, u32[]{:S(2)}) async-start(bf16[32,96,512]{2,1,0:T(8,128)(2,1)} %get-tuple-element.7), calls=%async_computation.1 | async-start | bytes 6291456 | tf_op jit(solution)/shard_map/all_to_all | solution.py:65
  83.8 143.9 %reduce-scatter.2.cloned.1.call-start = ((), (), s32[]{:S(2)}) async-start(), calls=%async_computation.5 | async-start | bytes 4456448 | tf_op jit(solution)/shard_map/reduce_scatter | solution.py:96
  132.0 1.7 copy-start.1
  146.1 0.7 copy-start.9
  146.1 81.5 %copy-start.3 = (bf16[1,64,512]{2,1,0:T(8,128)(2,1)S(1)}, bf16[1,64,512]{2,1,0:T(8,128)(2,1)}, u32[]{:S(2)}) copy-start(bf16[1,64,512]{2,1,0:T(8,128)(2,1)} %param.17) | copy-start | bytes 196612
  146.1 81.5 %copy-start.4 = (bf16[1,64,512]{2,1,0:T(8,128)(2,1)S(1)}, bf16[1,64,512]{2,1,0:T(8,128)(2,1)}, u32[]{:S(2)}) copy-start(bf16[1,64,512]{2,1,0:T(8,128)(2,1)} %param.16) | copy-start | bytes 196612
  146.1 81.5 %copy-start.5 = (bf16[1,64,512]{2,1,0:T(8,128)(2,1)S(1)}, bf16[1,64,512]{2,1,0:T(8,128)(2,1)}, u32[]{:S(2)}) copy-start(bf16[1,64,512]{2,1,0:T(8,128)(2,1)} %param.15) | copy-start | bytes 196612
  146.2 81.5 %copy-start.6 = (bf16[1,64,512]{2,1,0:T(8,128)(2,1)S(1)}, bf16[1,64,512]{2,1,0:T(8,128)(2,1)}, u32[]{:S(2)}) copy-start(bf16[1,64,512]{2,1,0:T(8,128)(2,1)} %param.14) | copy-start | bytes 196612
  147.5 11.3 %all-to-all-start.2 = ((f32[32,1,6]{2,1,0:T(1,128)}), f32[32,1,6]{2,1,0:T(1,128)S(1)}, u32[]{:S(2)}, u32[]{:S(2)}) async-start(f32[32,1,6]{2,1,0:T(1,128)} %bitcast.14), calls=%async_computation.3 | async-start | bytes 32768 | tf_op jit(solution)/shard_map/all_to_all | solution.py:102
Sparse Core Ops, SparseCore 0:
  40.6 74.9 all-gather.1
  146.3 81.2 reduce-scatter.1

commit v6 on v5

--- a/solution.py
+++ b/solution.py
@@ -13,7 +13,7 @@
     return first_new / (jnp.sqrt(second_new) + adam_eps)
 
 
-def body(
+def step(
     tokens,
     residual,
     token_adapter_index,
@@ -57,9 +57,10 @@
         return picked.reshape(owner_count, slot_capacity * pieces, piece)
 
     def send(row_block):
-        return lax.all_to_all(place(row_block), "owner", split_axis=0, concat_axis=0, tiled=True)
+        return lax.all_to_all(row_block, "owner", split_axis=0, concat_axis=0, tiled=True)
 
-    arrived_tokens = send(tokens)
+    placed_tokens = place(tokens)
+    arrived_tokens = send(placed_tokens)
     placed_residual, arrived_tokens = lax.optimization_barrier((place(residual), arrived_tokens))
     arrived = arrived_tokens.reshape(slots, width)
     arrived_residual = lax.all_to_all(
@@ -112,7 +113,7 @@
 
 def solution(mesh):
     return jax.shard_map(
-        body,
+        step,
         mesh=mesh,
         in_specs=(
             P(("dp", "owner"), None),

time: 237 us -> 237 us (level)
  no operation moved by 1% of the time
where the time goes in v6:
time: 237 us; the launch traced here: 236 us
  waiting for transfers between devices  140 us (59%)
  local copies, waits for them, and re-layouts  28.5 us (12%)
  starting transfers between devices  22.6 us (10%)
  other arithmetic  16.5 us (7%)
  matrix products  14.3 us (6%)
  between operations  14.2 us (6%)
    reduce_scatter x1, waiting for transfers between devices, step(): summed = lax.psum_scatter(both_grads, 'dp', scatter_dimension=1, tiled=True)  65.7 us
    all_to_all x1, waiting for transfers between devices, send(): lax.all_to_all(row_block, 'owner', split_axis=0, concat_axis=0, tiled=True)  37.4 us
    all_gather x1, waiting for transfers between devices, step(): both_full = lax.all_gather(both_weights, 'dp', axis=1, tiled=True)  27.5 us
    all_to_all x1, starting transfers between devices, send(): lax.all_to_all(row_block, 'owner', split_axis=0, concat_axis=0, tiled=True)  9.83 us
    unnamed x22, local copies, waits for them, and re-layouts  8.61 us
    gather x2, local copies, waits for them, and re-layouts, place(): split_rows[source]  6.9 us
    all_to_all x1, starting transfers between devices, step(): lax.all_to_all(placed_residual, 'owner', split_axis=0, concat_axis=0, til...  6.75 us
    all_to_all x1, starting transfers between devices, step(): lax.all_to_all(slot_loss.reshape(owner_count, slot_capacity), 'owner', sp...  5.9 us
  transfers between devices with their start and end apart: 5, of which 5 were waited for; matrix products, arithmetic and copies ran while one was open for 5% of the time, Pallas kernels for 0%

profile of v6, /device:TPU:6, one launch (start us, length us, event | category | flops | bytes accessed | tf_op | source)
XLA Modules:
  0.0 236.3 jit_solution(3586301800810176762)
XLA Ops:
  8.1 1.0 select_reduce_fusion
  10.5 3.8 %copy.20 = bf16[16,8,16,512]{3,2,1,0:T(8,128)(2,1)} copy(bf16[16,8,16,512]{3,1,2,0:T(8,128)(2,1)} %bitcast.48) | data formatting | bytes 4194304
  15.1 4.3 %gather_fusion = bf16[192,16,512]{2,1,0:T(8,128)(2,1)} fusion(bf16[128,16,512]{2,1,0:T(8,128)(2,1)} %bitcast.45, s32[1024]{0:T(1024)S(1)} %pad_clamp_fusion.1), kind=kCustom, calls=%fused_computation | custom fusion | bytes 6292224 | tf_op jit(solution)/shard_map/gather | solution.py:56
  19.4 2.6 %gather_fusion.1 = bf16[192,16,512]{2,1,0:T(8,128)(2,1)} fusion(bf16[128,16,512]{2,1,0:T(8,128)(2,1)S(1)} %bitcast.44, s32[1024]{0:T(1024)S(1)} %pad_clamp_fusion.1), kind=kCustom, calls=%fused_computation.1 | custom fusion | bytes 6292224 | tf_op jit(solution)/shard_map/gather | solution.py:56
  22.4 4.9 %bitcast_select_fusion = (bf16[32,96,512]{2,1,0:T(8,128)(2,1)}, bf16[32,96,512]{2,1,0:T(8,128)(2,1)}) fusion(pred[32,96]{1,0:T(8,128)(4,1)S(1)} %copy.18, bf16[32,96,512]{2,1,0:T(8,128)(2,1)} %bitcast.47, bf16[32,96,512]{2,1,0:T(8,128)(2,1)} %bitcast.46), kind=kLoop, calls=%fused_computation.11 | loop fusion | flops 3145728 | bytes 12585984 | tf_op jit(solution)/shard_map/jit(_where)/select_n | solution.py:56
  27.3 9.8 %all-to-all-start = ((bf16[32,96,512]{2,1,0:T(8,128)(2,1)}), bf16[32,96,512]{2,1,0:T(8,128)(2,1)S(1)}, u32[]{:S(2)}, u32[]{:S(2)}) async-start(bf16[32,96,512]{2,1,0:T(8,128)(2,1)} %get-tuple-element.11), calls=%async_computation | async-start | bytes 6291456 | tf_op jit(solution)/shard_map/all_to_all | solution.py:60
  37.9 37.4 %all-to-all-done = bf16[32,96,512]{2,1,0:T(8,128)(2,1)S(1)} async-done(((bf16[32,96,512]{2,1,0:T(8,128)(2,1)}), bf16[32,96,512]{2,1,0:T(8,128)(2,1)S(1)}, u32[]{:S(2)}, u32[]{:S(2)}) %all-to-all-start) | async-done | bytes 3145760 | tf_op jit(solution)/shard_map/all_to_all | solution.py:60
  75.3 1.7 copy-done
  77.0 6.7 %all-to-all-start.1 = ((bf16[32,96,512]{2,1,0:T(8,128)(2,1)}), bf16[32,96,512]{2,1,0:T(8,128)(2,1)}, u32[]{:S(2)}, u32[]{:S(2)}) async-start(bf16[32,96,512]{2,1,0:T(8,128)(2,1)} %get-tuple-element.7), calls=%async_computation.1 | async-start | bytes 6291456 | tf_op jit(solution)/shard_map/all_to_all | solution.py:66
  83.8 4.2 %reshape.85 = bf16[192,8192]{1,0:T(8,128)(2,1)S(1)} reshape(bf16[32,96,512]{2,1,0:T(8,128)(2,1)} %copy-done) | data formatting | bytes 6291456 | tf_op jit(solution)/shard_map/reshape | solution.py:65
  88.0 27.5 %all-gather.2.cloned.1.call-done = bf16[128,8192]{1,0:T(8,128)(2,1)} async-done(((bf16[128,512]{1,0:T(8,128)(2,1)}), bf16[128,8192]{1,0:T(8,128)(2,1)}) %all-gather.2.cloned.1.call-update) | async-done | bytes 2097168 | tf_op jit(solution)/shard_map/all_gather | solution.py:50
  115.6 2.3 convolution_convert_fusion
  117.9 4.1 %all-to-all-done.1 = bf16[32,96,512]{2,1,0:T(8,128)(2,1)} async-done(((bf16[32,96,512]{2,1,0:T(8,128)(2,1)}), bf16[32,96,512]{2,1,0:T(8,128)(2,1)}, u32[]{:S(2)}, u32[]{:S(2)}) %all-to-all-start.1) | async-done | bytes 3145760 | tf_op jit(solution)/shard_map/all_to_all | solution.py:66
  122.0 5.9 %reshape.84 = bf16[192,8192]{1,0:T(8,128)(2,1)} reshape(bf16[32,96,512]{2,1,0:T(8,128)(2,1)} %all-to-all-done.1) | data formatting | bytes 6291456 | tf_op jit(solution)/shard_map/reshape | solution.py:69
  127.9 4.1 %fusion.3 = (f32[192]{0:T(256)S(1)}, bf16[192,8192]{1,0:T(8,128)(2,1)S(1)}) fusion(bf16[192,64]{0,1:T(8,128)(2,1)S(1)} %convolution_convert_fusion, bf16[128,8192]{1,0:T(8,128)(2,1)} %all-gather.2.cloned.1.call-done, bf16[192,8192]{1,0:T(8,128)(2,1)} %reshape.84), kind=kOutput, calls=%fused_computation.9 | convolution fusion | flops 215482176 | bytes 7365376 | tf_op jit(solution)/shard_map/dot_general | solution.py:75
  132.0 1.7 copy-done.1
  133.7 2.0 convolution_multiply_fusion.1
  135.7 5.9 %fusion.14 = f32[64,8192]{1,0:T(8,128)} fusion(bf16[192,8192]{1,0:T(8,128)(2,1)S(1)} %reshape.85, bf16[192,8192]{1,0:T(8,128)(2,1)} %copy-done.1, bf16[128,8192]{1,0:T(8,128)(2,1)} %all-gather.2.cloned.1.call-done), kind=kOutput, calls=%fused_computation.19 | convolution fusion | flops 402677760 | bytes 9437184 | tf_op jit(solution)/shard_map/dot_general | solution.py:92
  141.6 4.6 %pad_maximum_fusion = f32[128,8192]{1,0:T(8,128)} fusion(f32[64,8192]{1,0:T(8,128)} %convolution_multiply_fusion.1, f32[64,8192]{1,0:T(8,128)} %fusion.14), kind=kLoop, calls=%fused_computation.10 | loop fusion | flops 1048576 | bytes 8388608 | tf_op jit(solution)/shard_map/concatenate | solution.py:96
  147.5 5.9 %all-to-all-start.2 = ((f32[32,1,6]{2,1,0:T(1,128)}), f32[32,1,6]{2,1,0:T(1,128)S(1)}, u32[]{:S(2)}, u32[]{:S(2)}) async-start(f32[32,1,6]{2,1,0:T(1,128)} %bitcast.14), calls=%async_computation.3 | async-start | bytes 32768 | tf_op jit(solution)/shard_map/all_to_all | solution.py:103
  153.4 5.4 %all-to-all-done.2 = f32[32,1,6]{2,1,0:T(1,128)S(1)} async-done(((f32[32,1,6]{2,1,0:T(1,128)}), f32[32,1,6]{2,1,0:T(1,128)S(1)}, u32[]{:S(2)}, u32[]{:S(2)}) %all-to-all-start.2) | async-done | bytes 800 | tf_op jit(solution)/shard_map/all_to_all | solution.py:103
  160.2 1.3 gather_fusion.2
  161.9 65.7 %reduce-scatter.2.cloned.1.call-done = f32[128,512]{1,0:T(8,128)} async-done(((f32[128,8192]{1,0:T(8,128)}), f32[128,512]{1,0:T(8,128)}) %reduce-scatter.2.cloned.1.call-update) | async-done | bytes 262160 | tf_op jit(solution)/shard_map/reduce_scatter | solution.py:97
  227.6 1.8 fusion.29
  (44 shorter events, 7.4 us)
Async XLA Ops:
  8.1 6.2 %copy-start.2 = (bf16[128,8192]{1,0:T(8,128)(2,1)S(1)}, bf16[128,8192]{1,0:T(8,128)(2,1)}, u32[]{:S(2)}) copy-start(bf16[128,8192]{1,0:T(8,128)(2,1)} %param.9) | copy-start | bytes 6291460
  27.3 9.9 %copy-start.7 = (bf16[1,64,512]{2,1,0:T(8,128)(2,1)S(1)}, bf16[1,64,512]{2,1,0:T(8,128)(2,1)}, u32[]{:S(2)}) copy-start(bf16[1,64,512]{2,1,0:T(8,128)(2,1)} %param.13) | copy-start | bytes 196612
  27.3 9.9 %copy-start.8 = (bf16[1,64,512]{2,1,0:T(8,128)(2,1)S(1)}, bf16[1,64,512]{2,1,0:T(8,128)(2,1)}, u32[]{:S(2)}) copy-start(bf16[1,64,512]{2,1,0:T(8,128)(2,1)} %param.12) | copy-start | bytes 196612
  27.3 48.0 %all-to-all-start = ((bf16[32,96,512]{2,1,0:T(8,128)(2,1)}), bf16[32,96,512]{2,1,0:T(8,128)(2,1)S(1)}, u32[]{:S(2)}, u32[]{:S(2)}) async-start(bf16[32,96,512]{2,1,0:T(8,128)(2,1)} %get-tuple-element.11), calls=%async_computation | async-start | bytes 6291456 | tf_op jit(solution)/shard_map/all_to_all | solution.py:60
  37.1 78.5 %all-gather.2.cloned.1.call-start = ((), (), s32[]{:S(2)}) async-start(), calls=%async_computation.4 | async-start | bytes 2228224 | tf_op jit(solution)/shard_map/all_gather | solution.py:50
  75.3 1.7 copy-start
  77.0 45.0 %all-to-all-start.1 = ((bf16[32,96,512]{2,1,0:T(8,128)(2,1)}), bf16[32,96,512]{2,1,0:T(8,128)(2,1)}, u32[]{:S(2)}, u32[]{:S(2)}) async-start(bf16[32,96,512]{2,1,0:T(8,128)(2,1)} %get-tuple-element.7), calls=%async_computation.1 | async-start | bytes 6291456 | tf_op jit(solution)/shard_map/all_to_all | solution.py:66
  83.8 143.9 %reduce-scatter.2.cloned.1.call-start = ((), (), s32[]{:S(2)}) async-start(), calls=%async_computation.5 | async-start | bytes 4456448 | tf_op jit(solution)/shard_map/reduce_scatter | solution.py:97
  132.0 1.7 copy-start.1
  146.1 0.7 copy-start.9
  146.1 81.5 %copy-start.3 = (bf16[1,64,512]{2,1,0:T(8,128)(2,1)S(1)}, bf16[1,64,512]{2,1,0:T(8,128)(2,1)}, u32[]{:S(2)}) copy-start(bf16[1,64,512]{2,1,0:T(8,128)(2,1)} %param.17) | copy-start | bytes 196612
  146.1 81.5 %copy-start.4 = (bf16[1,64,512]{2,1,0:T(8,128)(2,1)S(1)}, bf16[1,64,512]{2,1,0:T(8,128)(2,1)}, u32[]{:S(2)}) copy-start(bf16[1,64,512]{2,1,0:T(8,128)(2,1)} %param.16) | copy-start | bytes 196612
  146.1 81.5 %copy-start.5 = (bf16[1,64,512]{2,1,0:T(8,128)(2,1)S(1)}, bf16[1,64,512]{2,1,0:T(8,128)(2,1)}, u32[]{:S(2)}) copy-start(bf16[1,64,512]{2,1,0:T(8,128)(2,1)} %param.15) | copy-start | bytes 196612
  146.2 81.5 %copy-start.6 = (bf16[1,64,512]{2,1,0:T(8,128)(2,1)S(1)}, bf16[1,64,512]{2,1,0:T(8,128)(2,1)}, u32[]{:S(2)}) copy-start(bf16[1,64,512]{2,1,0:T(8,128)(2,1)} %param.14) | copy-start | bytes 196612
  147.5 11.3 %all-to-all-start.2 = ((f32[32,1,6]{2,1,0:T(1,128)}), f32[32,1,6]{2,1,0:T(1,128)S(1)}, u32[]{:S(2)}, u32[]{:S(2)}) async-start(f32[32,1,6]{2,1,0:T(1,128)} %bitcast.14), calls=%async_computation.3 | async-start | bytes 32768 | tf_op jit(solution)/shard_map/all_to_all | solution.py:103
Sparse Core Ops, SparseCore 0:
  40.6 74.9 all-gather.1
  146.3 81.2 reduce-scatter.1

commit v7 on v3

--- a/solution.py
+++ b/solution.py
@@ -13,7 +13,7 @@
     return first_new / (jnp.sqrt(second_new) + adam_eps)
 
 
-def body(
+def step(
     tokens,
     residual,
     token_adapter_index,
@@ -56,11 +56,14 @@
         picked = jnp.where(valid[:, None, None], split_rows[source], jnp.zeros((), row_block.dtype))
         return picked.reshape(owner_count, slot_capacity * pieces, piece)
 
+    def send(row_block):
+        return lax.all_to_all(row_block, "owner", split_axis=0, concat_axis=0, tiled=True)
+
     placed = jnp.concatenate([place(tokens), place(residual)], axis=1)
-    arrived_both = lax.all_to_all(placed, "owner", split_axis=0, concat_axis=0, tiled=True)
+    arrived_both = send(placed)
     half = slot_capacity * pieces
-    arrived = arrived_both[:, :half].reshape(slots, width)
-    arrived_residual = arrived_both[:, half:].reshape(slots, width)
+    arrived = lax.optimization_barrier(arrived_both[:, :half].reshape(slots, width))
+    arrived_residual = lax.optimization_barrier(arrived_both[:, half:].reshape(slots, width))
 
     hidden_state = lax.dot_general(
         arrived, down_full, (((1,), (1,)), ((), ())), preferred_element_type=jnp.float32
@@ -107,7 +110,7 @@
 
 def solution(mesh):
     return jax.shard_map(
-        body,
+        step,
         mesh=mesh,
         in_specs=(
             P(("dp", "owner"), None),

time: 256 us -> 252 us (0.984)
  other arithmetic: 25.5 us -> 18.1 us
  local copies, waits for them, and re-layouts: 28.3 us -> 33.1 us
    convert_element_type x2 -> x1, other arithmetic: 8.32 us -> 0.74 us  [step(): (route_ids[:, None] == jnp.arange(owner_count, dtype=jnp.int32)[None, :])...]
    convert_element_type x1 -> x0, local copies, waits for them, and re-layouts: 7.18 us -> none  [body(): arrived_residual.astype(jnp.float32) + adapter_output.astype(jnp.float32)]
    slice x0 -> x1, local copies, waits for them, and re-layouts: none -> 6.25 us  [step(): arrived_both[:, half:].reshape(slots, width)]
    reshape x2 -> x3, local copies, waits for them, and re-layouts: 4.3 us -> 10.2 us  [the longest x1 5.9 us: step(): arrived_both[:, half:].reshape(slots, width)]
  transfers between devices with their start and end apart: 4 -> 4, of which waited for: 3 -> 3; matrix products, arithmetic and copies ran while one was open for 9% -> 8% of each run, Pallas kernels for 0% -> 0%
where the time goes in v7:
time: 252 us; the launch traced here: 251 us
  waiting for transfers between devices  148 us (59%)
  local copies, waits for them, and re-layouts  33.1 us (13%)
  starting transfers between devices  24.7 us (10%)
  other arithmetic  18.1 us (7%)
  between operations  14.2 us (6%)
  matrix products  13.6 us (5%)
    all_to_all x1, waiting for transfers between devices, send(): lax.all_to_all(row_block, 'owner', split_axis=0, concat_axis=0, tiled=True)  76.3 us
    reduce_scatter x1, waiting for transfers between devices, step(): summed = lax.psum_scatter(both_grads, 'dp', scatter_dimension=1, tiled=True)  66 us
    all_to_all x1, starting transfers between devices, step(): lax.all_to_all(slot_loss.reshape(owner_count, slot_capacity), 'owner', sp...  14 us
    all_to_all x1, starting transfers between devices, send(): lax.all_to_all(row_block, 'owner', split_axis=0, concat_axis=0, tiled=True)  10.6 us
    gather x2, local copies, waits for them, and re-layouts, place(): split_rows[source]  6.94 us
    unnamed x22, local copies, waits for them, and re-layouts  6.93 us
    slice x1, local copies, waits for them, and re-layouts, step(): arrived_both[:, half:].reshape(slots, width)  6.25 us
    reshape x1, local copies, waits for them, and re-layouts, step(): arrived_both[:, half:].reshape(slots, width)  5.9 us
  transfers between devices with their start and end apart: 4, of which 3 were waited for; matrix products, arithmetic and copies ran while one was open for 8% of the time, Pallas kernels for 0%

profile of v7, /device:TPU:6, one launch (start us, length us, event | category | flops | bytes accessed | tf_op | source)
XLA Modules:
  0.0 251.4 jit_solution(714365135325544665)
XLA Ops:
  7.2 0.7 fusion.32
  8.1 1.0 select_reduce_fusion
  10.5 3.8 %copy.21 = bf16[16,8,16,512]{3,2,1,0:T(8,128)(2,1)} copy(bf16[16,8,16,512]{3,1,2,0:T(8,128)(2,1)} %bitcast.48) | data formatting | bytes 4194304
  14.3 0.8 copy.20
  15.1 4.2 %gather_fusion.1 = bf16[192,16,512]{2,1,0:T(8,128)(2,1)} fusion(bf16[128,16,512]{2,1,0:T(8,128)(2,1)} %bitcast.45, s32[1024]{0:T(1024)S(1)} %pad_clamp_fusion.1), kind=kCustom, calls=%fused_computation.1 | custom fusion | bytes 6292224 | tf_op jit(solution)/shard_map/gather | solution.py:56
  19.4 2.7 %gather_fusion = bf16[192,16,512]{2,1,0:T(8,128)(2,1)} fusion(bf16[128,16,512]{2,1,0:T(8,128)(2,1)S(1)} %bitcast.44, s32[1024]{0:T(1024)S(1)} %pad_clamp_fusion.1), kind=kCustom, calls=%fused_computation | custom fusion | bytes 6292224 | tf_op jit(solution)/shard_map/gather | solution.py:56
  22.4 3.2 %bitcast_select_fusion.1 = (bf16[32,96,512]{2,1,0:T(8,128)(2,1)S(1)}, bf16[32,96,512]{2,1,0:T(8,128)(2,1)S(1)}) fusion(pred[32,96]{1,0:T(8,128)(4,1)S(1)} %copy.18, bf16[32,96,512]{2,1,0:T(8,128)(2,1)} %bitcast.47, bf16[32,96,512]{2,1,0:T(8,128)(2,1)} %bitcast.46), kind=kLoop, calls=%fused_computation.13 | loop fusion | flops 3145728 | bytes 12585984 | tf_op jit(solution)/shard_map/jit(_where)/select_n | solution.py:56
  25.6 3.3 %pad_maximum_fusion = bf16[32,192,512]{2,1,0:T(8,128)(2,1)} fusion(bf16[32,96,512]{2,1,0:T(8,128)(2,1)S(1)} %get-tuple-element.10, bf16[32,96,512]{2,1,0:T(8,128)(2,1)S(1)} %get-tuple-element.9), kind=kLoop, calls=%fused_computation.10 | loop fusion | flops 12582912 | bytes 12582912 | tf_op jit(solution)/shard_map/concatenate | solution.py:62
  28.9 10.6 %all-to-all-start = ((bf16[32,192,512]{2,1,0:T(8,128)(2,1)}), bf16[32,192,512]{2,1,0:T(8,128)(2,1)}, u32[]{:S(2)}, u32[]{:S(2)}) async-start(bf16[32,192,512]{2,1,0:T(8,128)(2,1)} %pad_maximum_fusion), calls=%async_computation | async-start | bytes 12582912 | tf_op jit(solution)/shard_map/all_to_all | solution.py:60
  40.3 76.3 %all-to-all-done = bf16[32,192,512]{2,1,0:T(8,128)(2,1)} async-done(((bf16[32,192,512]{2,1,0:T(8,128)(2,1)}), bf16[32,192,512]{2,1,0:T(8,128)(2,1)}, u32[]{:S(2)}, u32[]{:S(2)}) %all-to-all-start) | async-done | bytes 6291488 | tf_op jit(solution)/shard_map/all_to_all | solution.py:60
  116.7 6.3 %fusion.35 = (bf16[32,96,512]{2,1,0:T(8,128)(2,1)}, bf16[32,96,512]{2,1,0:T(8,128)(2,1)}) fusion(bf16[32,192,512]{2,1,0:T(8,128)(2,1)} %all-to-all-done), kind=kLoop, calls=%fused_computation.57 | loop fusion | bytes 12582912 | tf_op jit(solution)/shard_map/slice | solution.py:66
  122.9 4.2 %reshape.85 = bf16[192,8192]{1,0:T(8,128)(2,1)S(1)} reshape(bf16[32,96,512]{2,1,0:T(8,128)(2,1)} %get-tuple-element.6) | data formatting | bytes 6291456 | tf_op jit(solution)/shard_map/reshape | solution.py:65
  127.1 5.9 %reshape.84 = bf16[192,8192]{1,0:T(8,128)(2,1)} reshape(bf16[32,96,512]{2,1,0:T(8,128)(2,1)} %get-tuple-element.5) | data formatting | bytes 6291456 | tf_op jit(solution)/shard_map/reshape | solution.py:66
  133.0 2.5 convolution_convert_fusion
  135.5 3.1 %fusion.3 = (f32[192]{0:T(256)S(1)}, bf16[192,8192]{1,0:T(8,128)(2,1)S(1)}) fusion(bf16[192,64]{0,1:T(8,128)(2,1)S(1)} %convolution_convert_fusion, bf16[128,8192]{1,0:T(8,128)(2,1)} %all-gather.2.cloned.1.call-done, bf16[192,8192]{1,0:T(8,128)(2,1)S(1)} %copy-done.1), kind=kOutput, calls=%fused_computation.9 | convolution fusion | flops 215482176 | bytes 7365376 | tf_op jit(solution)/shard_map/dot_general | solution.py:72
  138.7 1.7 copy-done
  140.3 2.0 convolution_multiply_fusion.1
  142.4 5.9 %fusion.14 = f32[64,8192]{1,0:T(8,128)} fusion(bf16[192,8192]{1,0:T(8,128)(2,1)S(1)} %reshape.85, bf16[192,8192]{1,0:T(8,128)(2,1)} %copy-done, bf16[128,8192]{1,0:T(8,128)(2,1)} %all-gather.2.cloned.1.call-done), kind=kOutput, calls=%fused_computation.20 | convolution fusion | flops 402677760 | bytes 9437184 | tf_op jit(solution)/shard_map/dot_general | solution.py:89
  148.3 4.6 %pad_maximum_fusion.1 = f32[128,8192]{1,0:T(8,128)} fusion(f32[64,8192]{1,0:T(8,128)} %convolution_multiply_fusion.1, f32[64,8192]{1,0:T(8,128)} %fusion.14), kind=kLoop, calls=%fused_computation.11 | loop fusion | flops 1048576 | bytes 8388608 | tf_op jit(solution)/shard_map/concatenate | solution.py:93
  154.2 14.0 %all-to-all-start.1 = ((f32[32,1,6]{2,1,0:T(1,128)}), f32[32,1,6]{2,1,0:T(1,128)S(1)}, u32[]{:S(2)}, u32[]{:S(2)}) async-start(f32[32,1,6]{2,1,0:T(1,128)} %bitcast.14), calls=%async_computation.2 | async-start | bytes 32768 | tf_op jit(solution)/shard_map/all_to_all | solution.py:100
  168.2 5.4 %all-to-all-done.1 = f32[32,1,6]{2,1,0:T(1,128)S(1)} async-done(((f32[32,1,6]{2,1,0:T(1,128)}), f32[32,1,6]{2,1,0:T(1,128)S(1)}, u32[]{:S(2)}, u32[]{:S(2)}) %all-to-all-start.1) | async-done | bytes 800 | tf_op jit(solution)/shard_map/all_to_all | solution.py:100
  174.9 1.3 gather_fusion.2
  176.7 66.0 %reduce-scatter.2.cloned.1.call-done = f32[128,512]{1,0:T(8,128)} async-done(((f32[128,8192]{1,0:T(8,128)}), f32[128,512]{1,0:T(8,128)}) %reduce-scatter.2.cloned.1.call-update) | async-done | bytes 262160 | tf_op jit(solution)/shard_map/reduce_scatter | solution.py:94
  242.7 1.8 fusion.29
  (44 shorter events, 5.9 us)
Async XLA Ops:
  8.1 6.2 %copy-start.2 = (bf16[128,8192]{1,0:T(8,128)(2,1)S(1)}, bf16[128,8192]{1,0:T(8,128)(2,1)}, u32[]{:S(2)}) copy-start(bf16[128,8192]{1,0:T(8,128)(2,1)} %param.9) | copy-start | bytes 6291460
  28.9 10.7 %copy-start.7 = (bf16[1,64,512]{2,1,0:T(8,128)(2,1)S(1)}, bf16[1,64,512]{2,1,0:T(8,128)(2,1)}, u32[]{:S(2)}) copy-start(bf16[1,64,512]{2,1,0:T(8,128)(2,1)} %param.13) | copy-start | bytes 196612
  28.9 10.7 %copy-start.8 = (bf16[1,64,512]{2,1,0:T(8,128)(2,1)S(1)}, bf16[1,64,512]{2,1,0:T(8,128)(2,1)}, u32[]{:S(2)}) copy-start(bf16[1,64,512]{2,1,0:T(8,128)(2,1)} %param.12) | copy-start | bytes 196612
  28.9 87.7 %all-to-all-start = ((bf16[32,192,512]{2,1,0:T(8,128)(2,1)}), bf16[32,192,512]{2,1,0:T(8,128)(2,1)}, u32[]{:S(2)}, u32[]{:S(2)}) async-start(bf16[32,192,512]{2,1,0:T(8,128)(2,1)} %pad_maximum_fusion), calls=%async_computation | async-start | bytes 12582912 | tf_op jit(solution)/shard_map/all_to_all | solution.py:60
  39.5 93.5 %all-gather.2.cloned.1.call-start = ((), (), s32[]{:S(2)}) async-start(), calls=%async_computation.3 | async-start | bytes 2228224 | tf_op jit(solution)/shard_map/all_gather | solution.py:50
  40.3 202.5 %reduce-scatter.2.cloned.1.call-start = ((), (), s32[]{:S(2)}) async-start(), calls=%async_computation.4 | async-start | bytes 4456448 | tf_op jit(solution)/shard_map/reduce_scatter | solution.py:94
  133.0 2.5 copy-start.1
  138.7 1.7 copy-start
  152.8 0.7 copy-start.9
  152.8 89.9 %copy-start.3 = (bf16[1,64,512]{2,1,0:T(8,128)(2,1)S(1)}, bf16[1,64,512]{2,1,0:T(8,128)(2,1)}, u32[]{:S(2)}) copy-start(bf16[1,64,512]{2,1,0:T(8,128)(2,1)} %param.17) | copy-start | bytes 196612
  152.8 89.9 %copy-start.4 = (bf16[1,64,512]{2,1,0:T(8,128)(2,1)S(1)}, bf16[1,64,512]{2,1,0:T(8,128)(2,1)}, u32[]{:S(2)}) copy-start(bf16[1,64,512]{2,1,0:T(8,128)(2,1)} %param.16) | copy-start | bytes 196612
  152.8 89.9 %copy-start.5 = (bf16[1,64,512]{2,1,0:T(8,128)(2,1)S(1)}, bf16[1,64,512]{2,1,0:T(8,128)(2,1)}, u32[]{:S(2)}) copy-start(bf16[1,64,512]{2,1,0:T(8,128)(2,1)} %param.15) | copy-start | bytes 196612
  152.8 89.9 %copy-start.6 = (bf16[1,64,512]{2,1,0:T(8,128)(2,1)S(1)}, bf16[1,64,512]{2,1,0:T(8,128)(2,1)}, u32[]{:S(2)}) copy-start(bf16[1,64,512]{2,1,0:T(8,128)(2,1)} %param.14) | copy-start | bytes 196612
  154.2 19.4 %all-to-all-start.1 = ((f32[32,1,6]{2,1,0:T(1,128)}), f32[32,1,6]{2,1,0:T(1,128)S(1)}, u32[]{:S(2)}, u32[]{:S(2)}) async-start(f32[32,1,6]{2,1,0:T(1,128)} %bitcast.14), calls=%async_computation.2 | async-start | bytes 32768 | tf_op jit(solution)/shard_map/all_to_all | solution.py:100
Sparse Core Ops, SparseCore 0:
  43.0 74.0 all-gather.1
  153.0 89.7 reduce-scatter.1

commit v8 on v7

--- a/solution.py
+++ b/solution.py
@@ -61,9 +61,13 @@
 
     placed = jnp.concatenate([place(tokens), place(residual)], axis=1)
     arrived_both = send(placed)
-    half = slot_capacity * pieces
-    arrived = lax.optimization_barrier(arrived_both[:, :half].reshape(slots, width))
-    arrived_residual = lax.optimization_barrier(arrived_both[:, half:].reshape(slots, width))
+    both_rows = lax.optimization_barrier(
+        arrived_both.reshape(owner_count, 2, slot_capacity, pieces, piece)
+        .transpose(1, 0, 2, 3, 4)
+        .reshape(2, slots, width)
+    )
+    arrived = both_rows[0]
+    arrived_residual = both_rows[1]
 
     hidden_state = lax.dot_general(
         arrived, down_full, (((1,), (1,)), ((), ())), preferred_element_type=jnp.float32

time: 252 us -> 253 us (level)
    transpose x0 -> x1, local copies, waits for them, and re-layouts: none -> 6.75 us  [step(): both_rows = lax.optimization_barrier(arrived_both.reshape(owner_count, 2,...]
    slice x1 -> x0, local copies, waits for them, and re-layouts: 6.25 us -> none  [step(): arrived_both[:, half:].reshape(slots, width)]
    unnamed x22 -> x20, local copies, waits for them, and re-layouts: 6.93 us -> 5.26 us
    reshape x2 -> x1, local copies, waits for them, and re-layouts: 10.1 us -> 10.4 us  [step(): both_rows = lax.optimization_barrier(arrived_both.reshape(owner_count, 2,...]
  transfers between devices with their start and end apart: 4 -> 4, of which waited for: 3 -> 3; matrix products, arithmetic and copies ran while one was open for 8% -> 9% of each run, Pallas kernels for 0% -> 0%
where the time goes in v8:
time: 253 us; the launch traced here: 252 us
  waiting for transfers between devices  148 us (58%)
  local copies, waits for them, and re-layouts  32.3 us (13%)
  starting transfers between devices  24.7 us (10%)
  other arithmetic  18.1 us (7%)
  matrix products  15 us (6%)
  between operations  14.2 us (6%)
    all_to_all x1, waiting for transfers between devices, send(): lax.all_to_all(row_block, 'owner', split_axis=0, concat_axis=0, tiled=True)  76.3 us
    reduce_scatter x1, waiting for transfers between devices, step(): summed = lax.psum_scatter(both_grads, 'dp', scatter_dimension=1, tiled=True)  65.8 us
    all_to_all x1, starting transfers between devices, step(): lax.all_to_all(slot_loss.reshape(owner_count, slot_capacity), 'owner', sp...  14 us
    all_to_all x1, starting transfers between devices, send(): lax.all_to_all(row_block, 'owner', split_axis=0, concat_axis=0, tiled=True)  10.6 us
    reshape x1, local copies, waits for them, and re-layouts, step(): both_rows = lax.optimization_barrier(arrived_both.reshape(owner_count, 2,...  10.4 us
    gather x2, local copies, waits for them, and re-layouts, place(): split_rows[source]  6.94 us
    transpose x1, local copies, waits for them, and re-layouts, step(): both_rows = lax.optimization_barrier(arrived_both.reshape(owner_count, 2,...  6.75 us
    dot_general x1, matrix products, step(): lax.dot_general(hidden_gradient, arrived, (((0,), (0,)), ((), ())), prefe...  5.97 us
  transfers between devices with their start and end apart: 4, of which 3 were waited for; matrix products, arithmetic and copies ran while one was open for 9% of the time, Pallas kernels for 0%

profile of v8, /device:TPU:6, one launch (start us, length us, event | category | flops | bytes accessed | tf_op | source)
XLA Modules:
  0.0 251.8 jit_solution(16375203884813814411)
XLA Ops:
  7.2 0.7 fusion.34
  8.1 1.0 select_reduce_fusion
  10.5 3.8 %copy.24 = bf16[16,8,16,512]{3,2,1,0:T(8,128)(2,1)} copy(bf16[16,8,16,512]{3,1,2,0:T(8,128)(2,1)} %bitcast.62) | data formatting | bytes 4194304
  14.3 0.8 copy.23
  15.1 4.2 %gather_fusion.1 = bf16[192,16,512]{2,1,0:T(8,128)(2,1)} fusion(bf16[128,16,512]{2,1,0:T(8,128)(2,1)} %bitcast.59, s32[1024]{0:T(1024)S(1)} %pad_clamp_fusion.1), kind=kCustom, calls=%fused_computation.1 | custom fusion | bytes 6292224 | tf_op jit(solution)/shard_map/gather | solution.py:56
  19.4 2.7 %gather_fusion = bf16[192,16,512]{2,1,0:T(8,128)(2,1)} fusion(bf16[128,16,512]{2,1,0:T(8,128)(2,1)S(1)} %bitcast.58, s32[1024]{0:T(1024)S(1)} %pad_clamp_fusion.1), kind=kCustom, calls=%fused_computation | custom fusion | bytes 6292224 | tf_op jit(solution)/shard_map/gather | solution.py:56
  22.4 3.2 %bitcast_select_fusion.1 = (bf16[32,96,512]{2,1,0:T(8,128)(2,1)S(1)}, bf16[32,96,512]{2,1,0:T(8,128)(2,1)S(1)}) fusion(pred[32,96]{1,0:T(8,128)(4,1)S(1)} %copy.20, bf16[32,96,512]{2,1,0:T(8,128)(2,1)} %bitcast.61, bf16[32,96,512]{2,1,0:T(8,128)(2,1)} %bitcast.60), kind=kLoop, calls=%fused_computation.15 | loop fusion | flops 3145728 | bytes 12585984 | tf_op jit(solution)/shard_map/jit(_where)/select_n | solution.py:56
  25.6 3.3 %pad_maximum_fusion = bf16[32,192,512]{2,1,0:T(8,128)(2,1)} fusion(bf16[32,96,512]{2,1,0:T(8,128)(2,1)S(1)} %get-tuple-element.8, bf16[32,96,512]{2,1,0:T(8,128)(2,1)S(1)} %get-tuple-element.7), kind=kLoop, calls=%fused_computation.10 | loop fusion | flops 12582912 | bytes 12582912 | tf_op jit(solution)/shard_map/concatenate | solution.py:62
  28.9 10.6 %all-to-all-start = ((bf16[32,192,512]{2,1,0:T(8,128)(2,1)}), bf16[32,192,512]{2,1,0:T(8,128)(2,1)}, u32[]{:S(2)}, u32[]{:S(2)}) async-start(bf16[32,192,512]{2,1,0:T(8,128)(2,1)} %pad_maximum_fusion), calls=%async_computation | async-start | bytes 12582912 | tf_op jit(solution)/shard_map/all_to_all | solution.py:60
  40.3 76.3 %all-to-all-done = bf16[32,192,512]{2,1,0:T(8,128)(2,1)} async-done(((bf16[32,192,512]{2,1,0:T(8,128)(2,1)}), bf16[32,192,512]{2,1,0:T(8,128)(2,1)}, u32[]{:S(2)}, u32[]{:S(2)}) %all-to-all-start) | async-done | bytes 6291488 | tf_op jit(solution)/shard_map/all_to_all | solution.py:60
  116.7 6.7 %copy.21 = bf16[2,32,6,16,512]{4,3,2,1,0:T(8,128)(2,1)} copy(bf16[2,32,6,16,512]{4,3,2,0,1:T(8,128)(2,1)} %bitcast.6) | data formatting | bytes 12582912 | tf_op jit(solution)/shard_map/transpose | solution.py:66
  123.4 10.4 %reshape.87 = bf16[2,192,8192]{2,1,0:T(8,128)(2,1)} reshape(bf16[2,32,6,16,512]{4,3,2,1,0:T(8,128)(2,1)} %copy.21) | data formatting | bytes 12582912 | tf_op jit(solution)/shard_map/reshape | solution.py:67
  133.8 3.4 %fusion.15 = bf16[192,64]{0,1:T(8,128)(2,1)S(1)} fusion(bf16[2,192,8192]{2,1,0:T(8,128)(2,1)} %reshape.87, bf16[128,8192]{1,0:T(8,128)(2,1)} %all-gather.2.cloned.1.call-done), kind=kOutput, calls=%fused_computation.23 | convolution fusion | flops 201338880 | bytes 4218880 | tf_op jit(solution)/shard_map/dot_general | solution.py:72
  137.3 3.5 %fusion.3 = (f32[192]{0:T(256)S(1)}, bf16[192,8192]{1,0:T(8,128)(2,1)S(1)}) fusion(bf16[192,64]{0,1:T(8,128)(2,1)S(1)} %fusion.15, bf16[128,8192]{1,0:T(8,128)(2,1)S(1)} %copy-done.1, bf16[2,192,8192]{2,1,0:T(8,128)(2,1)} %reshape.87), kind=kOutput, calls=%fused_computation.9 | convolution fusion | flops 215482176 | bytes 7373568 | tf_op jit(solution)/shard_map/dot_general | solution.py:76
  140.8 2.1 convolution_multiply_fusion.1
  142.9 6.0 %fusion.4 = f32[64,8192]{1,0:T(8,128)} fusion(bf16[2,192,8192]{2,1,0:T(8,128)(2,1)} %reshape.87, bf16[192,8192]{1,0:T(8,128)(2,1)S(1)} %get-tuple-element.10, bf16[128,8192]{1,0:T(8,128)(2,1)} %all-gather.2.cloned.1.call-done), kind=kOutput, calls=%fused_computation.16 | convolution fusion | flops 402677760 | bytes 9437184 | tf_op jit(solution)/shard_map/dot_general | solution.py:93
  148.9 4.6 %pad_maximum_fusion.1 = f32[128,8192]{1,0:T(8,128)} fusion(f32[64,8192]{1,0:T(8,128)} %convolution_multiply_fusion.1, f32[64,8192]{1,0:T(8,128)} %fusion.4), kind=kLoop, calls=%fused_computation.11 | loop fusion | flops 1048576 | bytes 8388608 | tf_op jit(solution)/shard_map/concatenate | solution.py:97
  154.1 0.7 div.18
  154.8 14.0 %all-to-all-start.1 = ((f32[32,1,6]{2,1,0:T(1,128)}), f32[32,1,6]{2,1,0:T(1,128)S(1)}, u32[]{:S(2)}, u32[]{:S(2)}) async-start(f32[32,1,6]{2,1,0:T(1,128)} %bitcast.18), calls=%async_computation.2 | async-start | bytes 32768 | tf_op jit(solution)/shard_map/all_to_all | solution.py:104
  168.8 5.4 %all-to-all-done.1 = f32[32,1,6]{2,1,0:T(1,128)S(1)} async-done(((f32[32,1,6]{2,1,0:T(1,128)}), f32[32,1,6]{2,1,0:T(1,128)S(1)}, u32[]{:S(2)}, u32[]{:S(2)}) %all-to-all-start.1) | async-done | bytes 800 | tf_op jit(solution)/shard_map/all_to_all | solution.py:104
  174.7 0.7 reduce.23
  175.5 1.3 gather_fusion.2
  177.3 65.8 %reduce-scatter.2.cloned.1.call-done = f32[128,512]{1,0:T(8,128)} async-done(((f32[128,8192]{1,0:T(8,128)}), f32[128,512]{1,0:T(8,128)}) %reduce-scatter.2.cloned.1.call-update) | async-done | bytes 262160 | tf_op jit(solution)/shard_map/reduce_scatter | solution.py:98
  243.1 1.8 fusion.31
  (41 shorter events, 4.5 us)
Async XLA Ops:
  8.1 6.2 %copy-start = (bf16[128,8192]{1,0:T(8,128)(2,1)S(1)}, bf16[128,8192]{1,0:T(8,128)(2,1)}, u32[]{:S(2)}) copy-start(bf16[128,8192]{1,0:T(8,128)(2,1)} %param.9) | copy-start | bytes 6291460
  28.9 10.7 %copy-start.6 = (bf16[1,64,512]{2,1,0:T(8,128)(2,1)S(1)}, bf16[1,64,512]{2,1,0:T(8,128)(2,1)}, u32[]{:S(2)}) copy-start(bf16[1,64,512]{2,1,0:T(8,128)(2,1)} %param.13) | copy-start | bytes 196612
  28.9 10.7 %copy-start.7 = (bf16[1,64,512]{2,1,0:T(8,128)(2,1)S(1)}, bf16[1,64,512]{2,1,0:T(8,128)(2,1)}, u32[]{:S(2)}) copy-start(bf16[1,64,512]{2,1,0:T(8,128)(2,1)} %param.12) | copy-start | bytes 196612
  28.9 87.7 %all-to-all-start = ((bf16[32,192,512]{2,1,0:T(8,128)(2,1)}), bf16[32,192,512]{2,1,0:T(8,128)(2,1)}, u32[]{:S(2)}, u32[]{:S(2)}) async-start(bf16[32,192,512]{2,1,0:T(8,128)(2,1)} %pad_maximum_fusion), calls=%async_computation | async-start | bytes 12582912 | tf_op jit(solution)/shard_map/all_to_all | solution.py:60
  39.5 94.3 %all-gather.2.cloned.1.call-start = ((), (), s32[]{:S(2)}) async-start(), calls=%async_computation.3 | async-start | bytes 2228224 | tf_op jit(solution)/shard_map/all_gather | solution.py:50
  40.3 202.8 %reduce-scatter.2.cloned.1.call-start = ((), (), s32[]{:S(2)}) async-start(), calls=%async_computation.4 | async-start | bytes 4456448 | tf_op jit(solution)/shard_map/reduce_scatter | solution.py:98
  133.8 3.4 %copy-start.1 = (bf16[128,8192]{1,0:T(8,128)(2,1)S(1)}, bf16[128,8192]{1,0:T(8,128)(2,1)}, u32[]{:S(2)}) copy-start(bf16[128,8192]{1,0:T(8,128)(2,1)} %all-gather.2.cloned.1.call-done) | copy-start | bytes 6291460
  153.4 0.7 copy-start.8
  153.4 89.7 %copy-start.2 = (bf16[1,64,512]{2,1,0:T(8,128)(2,1)S(1)}, bf16[1,64,512]{2,1,0:T(8,128)(2,1)}, u32[]{:S(2)}) copy-start(bf16[1,64,512]{2,1,0:T(8,128)(2,1)} %param.17) | copy-start | bytes 196612
  153.4 89.7 %copy-start.3 = (bf16[1,64,512]{2,1,0:T(8,128)(2,1)S(1)}, bf16[1,64,512]{2,1,0:T(8,128)(2,1)}, u32[]{:S(2)}) copy-start(bf16[1,64,512]{2,1,0:T(8,128)(2,1)} %param.16) | copy-start | bytes 196612
  153.4 89.7 %copy-start.4 = (bf16[1,64,512]{2,1,0:T(8,128)(2,1)S(1)}, bf16[1,64,512]{2,1,0:T(8,128)(2,1)}, u32[]{:S(2)}) copy-start(bf16[1,64,512]{2,1,0:T(8,128)(2,1)} %param.15) | copy-start | bytes 196612
  153.4 89.7 %copy-start.5 = (bf16[1,64,512]{2,1,0:T(8,128)(2,1)S(1)}, bf16[1,64,512]{2,1,0:T(8,128)(2,1)}, u32[]{:S(2)}) copy-start(bf16[1,64,512]{2,1,0:T(8,128)(2,1)} %param.14) | copy-start | bytes 196612
  154.8 19.4 %all-to-all-start.1 = ((f32[32,1,6]{2,1,0:T(1,128)}), f32[32,1,6]{2,1,0:T(1,128)S(1)}, u32[]{:S(2)}, u32[]{:S(2)}) async-start(f32[32,1,6]{2,1,0:T(1,128)} %bitcast.18), calls=%async_computation.2 | async-start | bytes 32768 | tf_op jit(solution)/shard_map/all_to_all | solution.py:104
Sparse Core Ops, SparseCore 0:
  43.0 74.0 all-gather.1
  153.6 89.4 reduce-scatter.1

commit v9 on v8

--- a/solution.py
+++ b/solution.py
@@ -78,9 +78,6 @@
     shifted = arrived_residual.astype(jnp.float32) + adapter_output.astype(jnp.float32)
     slot_loss = jnp.mean(0.5 * shifted * shifted, axis=1)
     output_gradient = shifted.astype(jnp.bfloat16)
-    up_gradient = adapter_scale * lax.dot_general(
-        hidden_state, output_gradient, (((0,), (0,)), ((), ())), preferred_element_type=jnp.float32
-    )
     hidden_gradient = (
         adapter_scale
         * lax.dot_general(
@@ -90,11 +87,15 @@
             preferred_element_type=jnp.float32,
         )
     ).astype(jnp.bfloat16)
-    down_grad = lax.dot_general(
-        hidden_gradient, arrived, (((0,), (0,)), ((), ())), preferred_element_type=jnp.float32
+
+    right = both_rows.at[1].set(output_gradient)
+    left = jnp.stack([hidden_gradient, hidden_state])
+    both_grads = lax.dot_general(
+        left, right, (((1,), (1,)), ((0,), (0,))), preferred_element_type=jnp.float32
     )
+    both_grads = both_grads * jnp.array([1.0, adapter_scale], jnp.float32)[:, None, None]
+    both_grads = both_grads.reshape(2 * rank, width)
 
-    both_grads = jnp.concatenate([down_grad, up_gradient], axis=0)
     summed = lax.psum_scatter(both_grads, "dp", scatter_dimension=1, tiled=True)
     down_share = summed[:rank]
     up_share = summed[rank:]

time: 253 us -> 247 us (0.976)
  other arithmetic: 18.1 us -> 13.4 us
  matrix products: 15 us -> 12 us
    concatenate x1 -> x0, other arithmetic: 4.55 us -> none  [step(): both_grads = jnp.concatenate([down_grad, up_gradient], axis=0)]
    dot_general x2, matrix products: 8.03 us -> 4.34 us  [the longest x1 3.21 us: step(): lax.dot_general(left, right, (((1,), (1,)), ((0,), (0,))), preferred_elem...]
    unnamed x20 -> x26, local copies, waits for them, and re-layouts: 5.26 us -> 6.7 us
where the time goes in v9:
time: 247 us; the launch traced here: 246 us
  waiting for transfers between devices  148 us (60%)
  local copies, waits for them, and re-layouts  34 us (14%)
  starting transfers between devices  24.7 us (10%)
  between operations  14.2 us (6%)
  other arithmetic  13.4 us (5%)
  matrix products  12 us (5%)
    all_to_all x1, waiting for transfers between devices, send(): lax.all_to_all(row_block, 'owner', split_axis=0, concat_axis=0, tiled=True)  76.3 us
    reduce_scatter x1, waiting for transfers between devices, step(): summed = lax.psum_scatter(both_grads, 'dp', scatter_dimension=1, tiled=True)  66 us
    all_to_all x1, starting transfers between devices, step(): lax.all_to_all(slot_loss.reshape(owner_count, slot_capacity), 'owner', sp...  14 us
    all_to_all x1, starting transfers between devices, send(): lax.all_to_all(row_block, 'owner', split_axis=0, concat_axis=0, tiled=True)  10.6 us
    reshape x1, local copies, waits for them, and re-layouts, step(): both_rows = lax.optimization_barrier(arrived_both.reshape(owner_count, 2,...  10.4 us
    gather x2, local copies, waits for them, and re-layouts, place(): split_rows[source]  6.94 us
    transpose x1, local copies, waits for them, and re-layouts, step(): both_rows = lax.optimization_barrier(arrived_both.reshape(owner_count, 2,...  6.75 us
    unnamed x26, local copies, waits for them, and re-layouts  6.7 us
  transfers between devices with their start and end apart: 4, of which 3 were waited for; matrix products, arithmetic and copies ran while one was open for 9% of the time, Pallas kernels for 0%

profile of v9, /device:TPU:6, one launch (start us, length us, event | category | flops | bytes accessed | tf_op | source)
XLA Modules:
  0.0 246.2 jit_solution(4146828831917178941)
XLA Ops:
  7.2 0.7 fusion.35
  8.1 0.8 select_reduce_fusion
  10.7 3.9 %copy.24 = bf16[16,8,16,512]{3,2,1,0:T(8,128)(2,1)} copy(bf16[16,8,16,512]{3,1,2,0:T(8,128)(2,1)} %bitcast.69) | data formatting | bytes 4194304
  14.6 0.8 copy.25
  15.5 4.2 %gather_fusion = bf16[192,16,512]{2,1,0:T(8,128)(2,1)} fusion(bf16[128,16,512]{2,1,0:T(8,128)(2,1)} %bitcast.66, s32[1024]{0:T(1024)S(1)} %pad_clamp_fusion.1), kind=kCustom, calls=%fused_computation | custom fusion | bytes 6292224 | tf_op jit(solution)/shard_map/gather | solution.py:56
  19.7 2.7 %gather_fusion.1 = bf16[192,16,512]{2,1,0:T(8,128)(2,1)} fusion(bf16[128,16,512]{2,1,0:T(8,128)(2,1)S(1)} %bitcast.65, s32[1024]{0:T(1024)S(1)} %pad_clamp_fusion.1), kind=kCustom, calls=%fused_computation.1 | custom fusion | bytes 6292224 | tf_op jit(solution)/shard_map/gather | solution.py:56
  22.4 3.2 %bitcast_select_fusion.1 = (bf16[32,96,512]{2,1,0:T(8,128)(2,1)S(1)}, bf16[32,96,512]{2,1,0:T(8,128)(2,1)S(1)}) fusion(pred[32,96]{1,0:T(8,128)(4,1)S(1)} %copy.21, bf16[32,96,512]{2,1,0:T(8,128)(2,1)} %bitcast.67, bf16[32,96,512]{2,1,0:T(8,128)(2,1)} %bitcast.68), kind=kLoop, calls=%fused_computation.16 | loop fusion | flops 3145728 | bytes 12585984 | tf_op jit(solution)/shard_map/jit(_where)/select_n | solution.py:56
  25.6 3.3 %pad_maximum_fusion = bf16[32,192,512]{2,1,0:T(8,128)(2,1)} fusion(bf16[32,96,512]{2,1,0:T(8,128)(2,1)S(1)} %get-tuple-element.20, bf16[32,96,512]{2,1,0:T(8,128)(2,1)S(1)} %get-tuple-element.19), kind=kLoop, calls=%fused_computation.10 | loop fusion | flops 12582912 | bytes 12582912 | tf_op jit(solution)/shard_map/concatenate | solution.py:62
  28.9 10.6 %all-to-all-start = ((bf16[32,192,512]{2,1,0:T(8,128)(2,1)}), bf16[32,192,512]{2,1,0:T(8,128)(2,1)}, u32[]{:S(2)}, u32[]{:S(2)}) async-start(bf16[32,192,512]{2,1,0:T(8,128)(2,1)} %pad_maximum_fusion), calls=%async_computation | async-start | bytes 12582912 | tf_op jit(solution)/shard_map/all_to_all | solution.py:60
  40.3 76.3 %all-to-all-done = bf16[32,192,512]{2,1,0:T(8,128)(2,1)} async-done(((bf16[32,192,512]{2,1,0:T(8,128)(2,1)}), bf16[32,192,512]{2,1,0:T(8,128)(2,1)}, u32[]{:S(2)}, u32[]{:S(2)}) %all-to-all-start) | async-done | bytes 6291488 | tf_op jit(solution)/shard_map/all_to_all | solution.py:60
  116.7 6.7 %copy.22 = bf16[2,32,6,16,512]{4,3,2,1,0:T(8,128)(2,1)} copy(bf16[2,32,6,16,512]{4,3,2,0,1:T(8,128)(2,1)} %bitcast.6) | data formatting | bytes 12582912 | tf_op jit(solution)/shard_map/transpose | solution.py:66
  123.4 10.4 %reshape.123 = bf16[2,192,8192]{2,1,0:T(8,128)(2,1)} reshape(bf16[2,32,6,16,512]{4,3,2,1,0:T(8,128)(2,1)} %copy.22) | data formatting | bytes 12582912 | tf_op jit(solution)/shard_map/reshape | solution.py:67
  133.8 3.4 %fusion.13 = bf16[192,64]{0,1:T(8,128)(2,1)S(1)} fusion(bf16[2,192,8192]{2,1,0:T(8,128)(2,1)} %reshape.123, bf16[128,8192]{1,0:T(8,128)(2,1)} %all-gather.2.cloned.1.call-done), kind=kOutput, calls=%fused_computation.21 | convolution fusion | flops 201338880 | bytes 4218880 | tf_op jit(solution)/shard_map/dot_general | solution.py:72
  137.3 4.2 %fusion.3 = (f32[192]{0:T(256)S(1)}, bf16[192,8192]{1,0:T(8,128)(2,1)S(1)}) fusion(bf16[192,64]{0,1:T(8,128)(2,1)S(1)} %fusion.13, bf16[128,8192]{1,0:T(8,128)(2,1)} %all-gather.2.cloned.1.call-done, bf16[2,192,8192]{2,1,0:T(8,128)(2,1)} %reshape.123), kind=kOutput, calls=%fused_computation.9 | convolution fusion | flops 215482176 | bytes 7365376 | tf_op jit(solution)/shard_map/dot_general | solution.py:76
  141.9 1.3 copy-done.1
  143.1 1.1 fusion.14
  144.3 3.2 %convolution_multiply_fusion.1 = f32[2,64,8192]{2,1,0:T(8,128)} fusion(bf16[2,192,8192]{2,1,0:T(8,128)(2,1)S(1)} %bitcast_dynamic-update-slice_fusion, f32[2]{0:T(128)S(1)} %copy-done.9, bf16[1,192,64]{1,2,0:T(8,128)(2,1)S(1)} %bitcast.74, bf16[1,192,64]{1,2,0:T(8,128)(2,1)S(1)} %fusion.14), kind=kOutput, calls=%fused_computation.7 | convolution fusion | flops 403726336 | bytes 10534920 | tf_op jit(solution)/shard_map/dot_general | solution.py:93
  148.2 0.7 div.18
  148.9 14.0 %all-to-all-start.1 = ((f32[32,1,6]{2,1,0:T(1,128)}), f32[32,1,6]{2,1,0:T(1,128)S(1)}, u32[]{:S(2)}, u32[]{:S(2)}) async-start(f32[32,1,6]{2,1,0:T(1,128)} %bitcast.22), calls=%async_computation.2 | async-start | bytes 32768 | tf_op jit(solution)/shard_map/all_to_all | solution.py:105
  162.9 5.4 %all-to-all-done.1 = f32[32,1,6]{2,1,0:T(1,128)S(1)} async-done(((f32[32,1,6]{2,1,0:T(1,128)}), f32[32,1,6]{2,1,0:T(1,128)S(1)}, u32[]{:S(2)}, u32[]{:S(2)}) %all-to-all-start.1) | async-done | bytes 800 | tf_op jit(solution)/shard_map/all_to_all | solution.py:105
  168.8 0.7 reduce.25
  169.6 1.3 gather_fusion.2
  171.4 66.0 %reduce-scatter.2.cloned.1.call-done = f32[128,512]{1,0:T(8,128)} async-done(((f32[128,8192]{1,0:T(8,128)}), f32[128,512]{1,0:T(8,128)}) %reduce-scatter.2.cloned.1.call-update) | async-done | bytes 262160 | tf_op jit(solution)/shard_map/reduce_scatter | solution.py:99
  237.5 1.8 fusion.29
  (48 shorter events, 4.8 us)
Async XLA Ops:
  10.7 4.0 %copy-start = (bf16[128,8192]{1,0:T(8,128)(2,1)S(1)}, bf16[128,8192]{1,0:T(8,128)(2,1)}, u32[]{:S(2)}) copy-start(bf16[128,8192]{1,0:T(8,128)(2,1)} %param.13) | copy-start | bytes 6291460
  28.9 10.7 %copy-start.6 = (bf16[1,64,512]{2,1,0:T(8,128)(2,1)S(1)}, bf16[1,64,512]{2,1,0:T(8,128)(2,1)}, u32[]{:S(2)}) copy-start(bf16[1,64,512]{2,1,0:T(8,128)(2,1)} %param.16) | copy-start | bytes 196612
  28.9 10.7 %copy-start.7 = (bf16[1,64,512]{2,1,0:T(8,128)(2,1)S(1)}, bf16[1,64,512]{2,1,0:T(8,128)(2,1)}, u32[]{:S(2)}) copy-start(bf16[1,64,512]{2,1,0:T(8,128)(2,1)} %param.15) | copy-start | bytes 196612
  28.9 87.7 %all-to-all-start = ((bf16[32,192,512]{2,1,0:T(8,128)(2,1)}), bf16[32,192,512]{2,1,0:T(8,128)(2,1)}, u32[]{:S(2)}, u32[]{:S(2)}) async-start(bf16[32,192,512]{2,1,0:T(8,128)(2,1)} %pad_maximum_fusion), calls=%async_computation | async-start | bytes 12582912 | tf_op jit(solution)/shard_map/all_to_all | solution.py:60
  39.5 94.3 %all-gather.2.cloned.1.call-start = ((), (), s32[]{:S(2)}) async-start(), calls=%async_computation.3 | async-start | bytes 2228224 | tf_op jit(solution)/shard_map/all_gather | solution.py:50
  40.3 197.2 %reduce-scatter.2.cloned.1.call-start = ((), (), s32[]{:S(2)}) async-start(), calls=%async_computation.4 | async-start | bytes 4456448 | tf_op jit(solution)/shard_map/reduce_scatter | solution.py:99
  133.8 7.7 %slice-start = ((s8[6291456]{0:T(1024)(128)(4,1)}), s8[4194304]{0:T(1024)(128)(4,1)S(1)}, s32[]{:S(2)}) async-start(s8[6291456]{0:T(1024)(128)(4,1)} %bitcast.63), calls=%async_computation.5 | async-start | bytes 8388608
  137.3 4.2 %slice-start.1 = ((s8[6291456]{0:T(1024)(128)(4,1)}), s8[2097152]{0:T(1024)(128)(4,1)S(1)}, s32[]{:S(2)}) async-start(s8[6291456]{0:T(1024)(128)(4,1)} %bitcast.63), calls=%async_computation.6 | async-start | bytes 4194304
  141.5 1.6 copy-start.1
  143.1 1.1 copy-start.9
  147.5 0.7 copy-start.8
  147.5 90.0 %copy-start.2 = (bf16[1,64,512]{2,1,0:T(8,128)(2,1)S(1)}, bf16[1,64,512]{2,1,0:T(8,128)(2,1)}, u32[]{:S(2)}) copy-start(bf16[1,64,512]{2,1,0:T(8,128)(2,1)} %param.20) | copy-start | bytes 196612
  147.5 90.0 %copy-start.3 = (bf16[1,64,512]{2,1,0:T(8,128)(2,1)S(1)}, bf16[1,64,512]{2,1,0:T(8,128)(2,1)}, u32[]{:S(2)}) copy-start(bf16[1,64,512]{2,1,0:T(8,128)(2,1)} %param.19) | copy-start | bytes 196612
  147.5 90.0 %copy-start.4 = (bf16[1,64,512]{2,1,0:T(8,128)(2,1)S(1)}, bf16[1,64,512]{2,1,0:T(8,128)(2,1)}, u32[]{:S(2)}) copy-start(bf16[1,64,512]{2,1,0:T(8,128)(2,1)} %param.18) | copy-start | bytes 196612
  147.5 90.0 %copy-start.5 = (bf16[1,64,512]{2,1,0:T(8,128)(2,1)S(1)}, bf16[1,64,512]{2,1,0:T(8,128)(2,1)}, u32[]{:S(2)}) copy-start(bf16[1,64,512]{2,1,0:T(8,128)(2,1)} %param.17) | copy-start | bytes 196612
  148.9 19.5 %all-to-all-start.1 = ((f32[32,1,6]{2,1,0:T(1,128)}), f32[32,1,6]{2,1,0:T(1,128)S(1)}, u32[]{:S(2)}, u32[]{:S(2)}) async-start(f32[32,1,6]{2,1,0:T(1,128)} %bitcast.22), calls=%async_computation.2 | async-start | bytes 32768 | tf_op jit(solution)/shard_map/all_to_all | solution.py:105
Sparse Core Ops, SparseCore 0:
  43.0 74.0 all-gather.1
  147.7 89.7 reduce-scatter.1
